TPU v7x, 256 devices: a whole 4x4x8 slice. The times are simulated.
256 devices in a mesh: band: 16 (over x, y_lo, core), dom: 16 (over z, y_hi).
Axes of the slice: x: 4, y: 4 (y_hi: 2, y_lo: 2; y = y_hi * 2 + y_lo), z: 8, core: 2. Of those that a mesh axis runs over, the one named last changes fastest.
Arguments:
- psi: float32 [1024, 64, 8, 128], P('band', 'dom'), may hold values from -6 to 6
- potential: float32 [64, 8, 128], P('dom'), may hold values from -1 to 1
- owner: int32 [1], replicated, may hold values from 0 to 15
Outputs:
- filtered: float32 [1024, 64, 8, 128], P('band', 'dom')
- intersection: float32 [64, 1024], P(None, 'band')
- hamiltonian: float32 [64, 1024], P(None, 'band')
Inputs may be any that keep to these rules, and one draw needn't show every extreme that they name: The owner's panel holds bands 64 * owner to 64 * owner + 63.
All inputs are finite; a program needn't handle non-finite values.
Results may differ from a plain program's by a relative error of at most 0.000084.
Values sent between devices are 32-bit elements; how exact they have to be, the bound alone decides.
No kernel may reach another device: no remote copies, remote signals or barrier semaphores. Data moves between devices by JAX's collectives and lax.ppermute only.
A program may use at most 64 MiB of HBM per device.

v0:
```python
import jax
import jax.numpy as jnp
from jax import lax
from jax.sharding import PartitionSpec as P

center = 4.9
halfwidth = 4.1


def extended_2(block, sides, width):
    for axis, dim in sides:
        count = lax.axis_size(axis)
        forward = [(i, i + 1) for i in range(count - 1)]
        forward.append((count - 1, 0))
        backward = [(target, source) for source, target in forward]
        low = lax.ppermute(
            lax.slice_in_dim(block, block.shape[dim] - width, None, axis=dim), axis, forward
        )
        high = lax.ppermute(lax.slice_in_dim(block, 0, width, axis=dim), axis, backward)
        block = jnp.concatenate([low, block, high], axis=dim)
    return block


def broadcast(array, axis, root):
    mine = lax.axis_index(axis) == root
    return lax.psum(jnp.where(mine, array, jnp.zeros_like(array)), axis)


def lap_periodic(grid_field, which_axis):
    outer = jnp.roll(grid_field, 2, which_axis) + jnp.roll(grid_field, -2, which_axis)
    nearer = jnp.roll(grid_field, 1, which_axis) + jnp.roll(grid_field, -1, which_axis)
    return -1.0 / 12.0 * outer + 4.0 / 3.0 * nearer - 2.5 * grid_field


def hamiltonian_apply(extended, local_potential):
    interior = extended[:, 2:-2]
    along_first = (
        -1.0 / 12.0 * (extended[:, :-4] + extended[:, 4:])
        + 4.0 / 3.0 * (extended[:, 1:-3] + extended[:, 3:-1])
        - 2.5 * interior
    )
    laplace = along_first + lap_periodic(interior, 2) + lap_periodic(interior, 3)
    return -0.5 * laplace + local_potential * interior


def shifted(extended, local_potential):
    return (hamiltonian_apply(extended, local_potential) - center * extended[:, 2:-2]) / halfwidth


def with_faces(grid_field):
    return extended_2(grid_field, (("dom", 1),), 2)


def body(psi, potential, owner):
    current = psi
    first_term = shifted(with_faces(current), potential)
    current = 2.0 * shifted(with_faces(first_term), potential) - current
    local_bands = current.shape[0]
    owner_root = owner[0]
    owned_panel = broadcast(current, "band", owner_root)
    total_cells = current.shape[1] * current.shape[2] * current.shape[3] * lax.axis_size("dom")
    scale = 1.0 / total_cells
    flattened = current.reshape(local_bands, -1)
    panel_flat = owned_panel.reshape(local_bands, -1)
    extended = extended_2(current, (("dom", 1),), 2)
    applied = hamiltonian_apply(extended, potential)
    ham_rows = jnp.einsum(
        "pc,bc->pb", panel_flat, applied.reshape(local_bands, -1), precision=lax.Precision.HIGHEST
    )
    over_rows = jnp.einsum("pc,bc->pb", panel_flat, flattened, precision=lax.Precision.HIGHEST)
    intersection, hamiltonian = lax.psum((over_rows * scale, ham_rows * scale), "dom")
    return (current, intersection, hamiltonian)


def solution(mesh):
    placed = (P("band", "dom", None, None), P("dom", None, None), P())
    return jax.shard_map(
        body,
        mesh=mesh,
        in_specs=placed,
        out_specs=(P("band", "dom", None, None), P(None, "band"), P(None, "band")),
        check_vma=False,
    )
```

profile of v0, /device:TPU:0, one launch (start us, length us, event | category | flops | bytes accessed | tf_op | source)
XLA Modules:
  0.0 314.2 jit_solution(11371170364938100870)
XLA Ops:
  7.2 1.3 fusion.122
  8.5 1.0 copy.37
  9.5 6.8 %collective-permute-start.1 = (f32[64,2,8,128]{3,0,2,1:T(8,128)}, f32[64,2,8,128]{3,0,2,1:T(8,128)}, u32[]{:S(2)}, u32[]{:S(2)}) collective-permute-start(f32[64,2,8,128]{3,0,2,1:T(8,128)} %copy.37), channel_id=1, source_target_pairs={{1,0},{2,1},{3,2},{4,3},{5,4},{6,5},{7,6},{8,7},{9,8},{10,9},{11,1... | collective-permute-start | bytes 1572872 | tf_op jit(solution)/shard_map/ppermute | solution.py:19
  16.3 1.0 copy.38
  17.4 1.0 fusion.123
  18.4 1.3 fusion.126
  19.7 1.3 fusion.127
  21.0 1.7 fusion.128
  22.8 1.6 fusion.124
  24.3 1.7 fusion.129
  26.0 1.7 fusion.130
  28.5 0.7 copy.45
  29.1 1.0 copy.40
  30.1 1.7 copy.41
  31.8 1.5 copy.43
  33.3 1.5 copy.46
  35.4 0.6 copy.49
  36.6 1.6 copy.47
  38.2 1.6 copy.50
  39.8 1.4 copy.39
  41.3 1.3 copy.42
  42.6 1.6 copy.52
  44.2 1.6 copy.53
  45.8 1.6 copy.51
  47.4 1.6 copy.54
  49.0 1.2 constant_dynamic-update-slice_fusion.1
  50.2 0.6 constant_dynamic-update-slice_fusion
  50.8 1.4 constant_dynamic-update-slice_fusion.2
  52.5 4.1 %broadcast_multiply_fusion = (f32[64,4,8,128]{3,0,2,1:T(8,128)S(1)}, f32[64,4,8,128]{3,0,2,1:T(8,128)S(1)}) fusion(f32[4,8,128]{2,1,0:T(8,128)} %param.4, f32[64,4,8,1]{3,0,2,1:T(8,128)S(1)} %copy-done.4, f32[64,4,8,127]{3,0,2,1:T(8,128)} %copy.54, f32[64,4,8,127]{3,0,2,1:T(8,128)S(1)} %copy-done.5, f32[64,4,8,1]{3,0,2,1:T(8,128)S(1)} %copy-done.3, ...), kind=kLoop, calls=%fused_computation.115 | loop fusion | flops 9175040 | bytes 15745024 | tf_op jit(solution)/shard_map/div | solution.py:47
  58.4 5.7 %collective-permute-start.3 = (f32[64,2,8,128]{3,0,2,1:T(8,128)S(1)}, f32[64,2,8,128]{3,0,2,1:T(8,128)S(1)}, u32[]{:S(2)}, u32[]{:S(2)}) collective-permute-start(f32[64,2,8,128]{3,0,2,1:T(8,128)S(1)} %get-tuple-element.31), channel_id=1, source_target_pairs={{1,0},{2,1},{3,2},{4,3},{5,4},{6,5},{7,6},{8,7},{9,8},{10,9},{11,1... | collective-permute-start | bytes 1572872 | tf_op jit(solution)/shard_map/ppermute | solution.py:19
  64.6 16.3 %collective-permute-done.2 = f32[64,2,8,128]{3,0,2,1:T(8,128)S(1)} collective-permute-done((f32[64,2,8,128]{3,0,2,1:T(8,128)S(1)}, f32[64,2,8,128]{3,0,2,1:T(8,128)S(1)}, u32[]{:S(2)}, u32[]{:S(2)}) %collective-permute-start.2) | collective-permute-done | bytes 524320 | tf_op jit(solution)/shard_map/ppermute | solution.py:16
  80.8 3.8 %collective-permute-done.3 = f32[64,2,8,128]{3,0,2,1:T(8,128)S(1)} collective-permute-done((f32[64,2,8,128]{3,0,2,1:T(8,128)S(1)}, f32[64,2,8,128]{3,0,2,1:T(8,128)S(1)}, u32[]{:S(2)}, u32[]{:S(2)}) %collective-permute-start.3) | collective-permute-done | bytes 524320 | tf_op jit(solution)/shard_map/ppermute | solution.py:19
  84.6 3.6 %broadcast_select_fusion = (f32[64,4,8,128]{3,0,2,1:T(8,128)}, f32[64,4,8,128]{3,0,2,1:T(8,128)S(1)}) fusion(pred[]{:T(512)S(6)} %eq.3, f32[64,4,8,128]{3,2,1,0:T(8,128)S(1)} %copy-done, f32[64,4,8,128]{3,0,2,1:T(8,128)S(1)} %get-tuple-element.11, f32[4,8,128]{2,1,0:T(8,128)S(1)} %broadcast_multiply_fusion.1, f32[64,4,8,1]{3,0,2,1:T(8,128)S(1)} %get-tuple-element.45, ...), kind=kLoop, calls=%fused_computation.114 | loop fusion | flops 10747904 | bytes 14696449 | tf_op jit(solution)/shard_map/jit(_where)/select_n | solution.py:26
  88.2 1.1 fusion.112
  89.3 1.4 fusion.108
  90.7 1.3 fusion.106
  92.1 1.7 fusion.105
  93.8 1.7 fusion.107
  95.7 5.5 %collective-permute-start.5 = (f32[64,2,8,128]{3,0,2,1:T(8,128)}, f32[64,2,8,128]{3,0,2,1:T(8,128)}, u32[]{:S(2)}, u32[]{:S(2)}) collective-permute-start(f32[64,2,8,128]{3,0,2,1:T(8,128)} %get-tuple-element.29), channel_id=1, source_target_pairs={{1,0},{2,1},{3,2},{4,3},{5,4},{6,5},{7,6},{8,7},{9,8},{10,9},{11,1... | collective-permute-start | bytes 1572872 | tf_op jit(solution)/shard_map/ppermute | solution.py:19
  101.2 1.4 fusion.110
  102.6 1.7 fusion.104
  104.3 0.7 fusion.109
  105.0 1.6 copy.30
  106.6 0.7 fusion.111
  107.3 113.6 %all-reduce.3.cloned.1.call-done = f32[64,4,8,128]{3,0,2,1:T(8,128)} async-done(((f32[64,4,8,128]{3,0,2,1:T(8,128)}), f32[64,4,8,128]{3,0,2,1:T(8,128)}) %all-reduce.3.cloned.1.call-update) | async-done | bytes 1048592 | tf_op jit(solution)/shard_map/psum | solution.py:26
  220.9 2.3 fusion.1
  223.2 6.2 %fusion = f32[64,64]{1,0:T(8,128)S(1)} fusion(f32[64,4,8,128]{3,0,2,1:T(8,128)S(1)} %copy-done.16, f32[64,4,8,128]{3,0,2,1:T(8,128)S(1)} %get-tuple-element.9, f32[64,2,8,128]{3,0,2,1:T(8,128)} %collective-permute-done.5, f32[64,2,8,128]{3,0,2,1:T(8,128)} %collective-permute-done.4, f32[64,4,6,128]{3,0,2,1:T(8,128)} %get-tuple-element.25, ...), kind=kOutput, calls=%fused_computation.9 | convolution fusion | flops 210767872 | bytes 11567104 | tf_op jit(solution)/shard_map/pc,bc->pb/dot_general | solution.py:67
  229.5 77.9 %all-reduce = (f32[64,64]{1,0:T(8,128)}, f32[64,64]{1,0:T(8,128)}) all-reduce(f32[64,64]{1,0:T(8,128)S(1)} %fusion.1, f32[64,64]{1,0:T(8,128)S(1)} %fusion), channel_id=1, replica_groups=mesh['band'=16,'dom'=16] {'dom'}, use_global_device_ids=true, to_apply=%region_1.2 | all-reduce | flops 8192 | bytes 65536 | tf_op jit(solution)/shard_map/psum | solution.py:71
  (62 shorter events, 4.1 us)
Async XLA Ops:
  7.2 213.7 %all-reduce.3.cloned.1.call-start = ((), (), s32[]{:S(2)}) async-start(), calls=%async_computation | async-start | bytes 2097152 | tf_op jit(solution)/shard_map/psum | solution.py:26
  8.5 8.8 %copy-start = (f32[64,4,8,128]{3,2,1,0:T(8,128)S(1)}, f32[64,4,8,128]{3,2,1,0:T(8,128)}, u32[]{:S(2)}) copy-start(f32[64,4,8,128]{3,2,1,0:T(8,128)} %param.3) | copy-start | bytes 3145732
  9.5 41.3 %collective-permute-start.1 = (f32[64,2,8,128]{3,0,2,1:T(8,128)}, f32[64,2,8,128]{3,0,2,1:T(8,128)}, u32[]{:S(2)}, u32[]{:S(2)}) collective-permute-start(f32[64,2,8,128]{3,0,2,1:T(8,128)} %copy.37), channel_id=1, source_target_pairs={{1,0},{2,1},{3,2},{4,3},{5,4},{6,5},{7,6},{8,7},{9,8},{10,9},{11,1... | collective-permute-start | bytes 1572872 | tf_op jit(solution)/shard_map/ppermute | solution.py:19
  17.3 31.7 %collective-permute-start = (f32[64,2,8,128]{3,0,2,1:T(8,128)}, f32[64,2,8,128]{3,0,2,1:T(8,128)}, u32[]{:S(2)}, u32[]{:S(2)}) collective-permute-start(f32[64,2,8,128]{3,0,2,1:T(8,128)} %copy.38), channel_id=1, source_target_pairs={{0,1},{1,2},{2,3},{3,4},{4,5},{5,6},{6,7},{7,8},{8,9},{9,10},{10,1... | collective-permute-start | bytes 1572872 | tf_op jit(solution)/shard_map/ppermute | solution.py:16
  26.0 1.7 copy-start.18
  27.7 4.2 %copy-start.15 = (f32[64,4,7,128]{3,2,1,0:T(8,128)S(1)}, f32[64,4,7,128]{3,2,1,0:T(8,128)}, u32[]{:S(2)}) copy-start(f32[64,4,7,128]{3,2,1,0:T(8,128)} %get-tuple-element.58) | copy-start | bytes 2752516
  33.3 2.1 copy-start.14
  35.4 1.2 copy-start.13
  36.0 2.2 copy-start.12
  38.2 1.6 copy-start.7
  38.2 3.0 copy-start.6
  39.8 2.8 copy-start.11
  41.3 2.9 copy-start.10
  44.2 1.6 copy-start.9
  45.8 1.6 copy-start.8
  49.0 3.3 %copy-start.5 = (f32[64,4,8,127]{3,0,2,1:T(8,128)S(1)}, f32[64,4,8,127]{3,0,2,1:T(8,128)}, u32[]{:S(2)}) copy-start(f32[64,4,8,127]{3,0,2,1:T(8,128)} %copy.51) | copy-start | bytes 3121156
  50.1 2.1 copy-start.1
  50.1 2.1 copy-start.2
  50.2 2.1 copy-start.3
  50.2 2.3 copy-start.4
  58.4 22.5 %collective-permute-start.2 = (f32[64,2,8,128]{3,0,2,1:T(8,128)S(1)}, f32[64,2,8,128]{3,0,2,1:T(8,128)S(1)}, u32[]{:S(2)}, u32[]{:S(2)}) collective-permute-start(f32[64,2,8,128]{3,0,2,1:T(8,128)S(1)} %get-tuple-element.30), channel_id=1, source_target_pairs={{0,1},{1,2},{2,3},{3,4},{4,5},{5,6},{6,7},{7,8},{8,9},{9,10},{10,1... | collective-permute-start | bytes 1572872 | tf_op jit(solution)/shard_map/ppermute | solution.py:16
  58.4 26.2 %collective-permute-start.3 = (f32[64,2,8,128]{3,0,2,1:T(8,128)S(1)}, f32[64,2,8,128]{3,0,2,1:T(8,128)S(1)}, u32[]{:S(2)}, u32[]{:S(2)}) collective-permute-start(f32[64,2,8,128]{3,0,2,1:T(8,128)S(1)} %get-tuple-element.31), channel_id=1, source_target_pairs={{1,0},{2,1},{3,2},{4,3},{5,4},{6,5},{7,6},{8,7},{9,8},{10,9},{11,1... | collective-permute-start | bytes 1572872 | tf_op jit(solution)/shard_map/ppermute | solution.py:19
  95.5 127.7 %collective-permute-start.4 = (f32[64,2,8,128]{3,0,2,1:T(8,128)}, f32[64,2,8,128]{3,0,2,1:T(8,128)}, u32[]{:S(2)}, u32[]{:S(2)}) collective-permute-start(f32[64,2,8,128]{3,0,2,1:T(8,128)} %get-tuple-element.28), channel_id=1, source_target_pairs={{0,1},{1,2},{2,3},{3,4},{4,5},{5,6},{6,7},{7,8},{8,9},{9,10},{10,1... | collective-permute-start | bytes 1572872 | tf_op jit(solution)/shard_map/ppermute | solution.py:16
  95.7 127.5 %collective-permute-start.5 = (f32[64,2,8,128]{3,0,2,1:T(8,128)}, f32[64,2,8,128]{3,0,2,1:T(8,128)}, u32[]{:S(2)}, u32[]{:S(2)}) collective-permute-start(f32[64,2,8,128]{3,0,2,1:T(8,128)} %get-tuple-element.29), channel_id=1, source_target_pairs={{1,0},{2,1},{3,2},{4,3},{5,4},{6,5},{7,6},{8,7},{9,8},{10,9},{11,1... | collective-permute-start | bytes 1572872 | tf_op jit(solution)/shard_map/ppermute | solution.py:19
  106.6 116.7 %copy-start.19 = (f32[4,8,128]{2,1,0:T(8,128)S(1)}, f32[4,8,128]{2,1,0:T(8,128)}, u32[]{:S(2)}) copy-start(f32[4,8,128]{2,1,0:T(8,128)} %param.4) | copy-start | bytes 49156
  220.9 2.3 copy-start.16
  220.9 2.4 copy-start.17
Sparse Core Ops, SparseCore 0:
  95.6 125.2 all-reduce.2
where the time goes:
time: 315 us; the launch traced here: 314 us
  waiting for transfers between devices  134 us (43%)
  blocking collectives  77.9 us (25%)
  local copies, waits for them, and re-layouts  53 us (17%)
  starting transfers between devices  18.3 us (6%)
  between operations  15.1 us (5%)
  matrix products  8.52 us (3%)
  other arithmetic  7.73 us (2%)
    psum x1, waiting for transfers between devices, broadcast(): return lax.psum(jnp.where(mine, array, jnp.zeros_like(array)), axis)  114 us
    psum x1, blocking collectives, body(): lax.psum((over_rows * scale, ham_rows * scale), 'dom')  77.9 us
    unnamed x60, local copies, waits for them, and re-layouts  25.5 us
    ppermute x3, starting transfers between devices, extended_2(): lax.ppermute(lax.slice_in_dim(block, 0, width, axis=dim), axis, backward)  18 us
    ppermute x3, waiting for transfers between devices, extended_2(): lax.ppermute(lax.slice_in_dim(block, block.shape[dim] - width, None, axis...  16.3 us
    slice x8, local copies, waits for them, and re-layouts, lap_periodic(): jnp.roll(grid_field, 2, which_axis) + jnp.roll(grid_field, -2, which_axis)  6.59 us
  transfers between devices with their start and end apart: 7, of which 3 were waited for; matrix products, arithmetic and copies ran while one was open for 13% of the time, Pallas kernels for 0%

commit v1 on v0

--- a/solution.py
+++ b/solution.py
@@ -22,8 +22,20 @@
 
 
 def broadcast(array, axis, root):
-    mine = lax.axis_index(axis) == root
-    return lax.psum(jnp.where(mine, array, jnp.zeros_like(array)), axis)
+    count = lax.axis_size(axis)
+    piece = array.shape[0] // count
+    spread = lax.all_to_all(array, axis, 0, 0, tiled=True)
+    mine = lax.dynamic_slice_in_dim(spread, root * piece, piece, 0)
+    return lax.all_gather(mine, axis, axis=0, tiled=True)
+
+
+def doubling_sum(array, axis):
+    count = lax.axis_size(axis)
+    step = 1
+    while step < count:
+        array = array + lax.ppermute(array, axis, [(i, i ^ step) for i in range(count)])
+        step *= 2
+    return array
 
 
 def lap_periodic(grid_field, which_axis):
@@ -68,8 +80,8 @@
         "pc,bc->pb", panel_flat, applied.reshape(local_bands, -1), precision=lax.Precision.HIGHEST
     )
     over_rows = jnp.einsum("pc,bc->pb", panel_flat, flattened, precision=lax.Precision.HIGHEST)
-    intersection, hamiltonian = lax.psum((over_rows * scale, ham_rows * scale), "dom")
-    return (current, intersection, hamiltonian)
+    both = doubling_sum(jnp.stack([over_rows * scale, ham_rows * scale]), "dom")
+    return (current, both[0], both[1])
 
 
 def solution(mesh):

time: 315 us -> 183 us (0.58)
  blocking collectives: 77.9 us -> 0 us
  waiting for transfers between devices: 134 us -> 69.4 us
  starting transfers between devices: 18.3 us -> 38.7 us
  local copies, waits for them, and re-layouts: 53 us -> 39.4 us
  other arithmetic: 7.73 us -> 12.5 us
    psum x1 -> x0, waiting for transfers between devices: 114 us -> none  [broadcast(): return lax.psum(jnp.where(mine, array, jnp.zeros_like(array)), axis)]
    psum x1 -> x0, blocking collectives: 77.9 us -> none  [body(): lax.psum((over_rows * scale, ham_rows * scale), 'dom')]
    unnamed x60 -> x25, local copies, waits for them, and re-layouts: 25.5 us -> 1.21 us
    all_gather x0 -> x1, waiting for transfers between devices: none -> 20.3 us  [broadcast(): return lax.all_gather(mine, axis, axis=0, tiled=True)]
    ppermute x0 -> x4, starting transfers between devices: none -> 13.1 us  [doubling_sum(): lax.ppermute(array, axis, [(i, i ^ step) for i in range(count)])]
    ppermute x3, waiting for transfers between devices: 16.3 us -> 28.1 us  [extended_2(): lax.ppermute(lax.slice_in_dim(block, block.shape[dim] - width, None, axis...]
    ppermute x0 -> x4, waiting for transfers between devices: none -> 11.1 us  [doubling_sum(): lax.ppermute(array, axis, [(i, i ^ step) for i in range(count)])]
    slice x4 -> x8, local copies, waits for them, and re-layouts: 5.15 us -> 11.6 us  [lap_periodic(): jnp.roll(grid_field, -2, which_axis)]
  transfers between devices with their start and end apart: 7 -> 12, of which waited for: 3 -> 12; matrix products, arithmetic and copies ran while one was open for 13% -> 21% of each run, Pallas kernels for 0% -> 0%
where the time goes in v1:
time: 183 us; the launch traced here: 181 us
  waiting for transfers between devices  69.4 us (38%)
  local copies, waits for them, and re-layouts  39.4 us (22%)
  starting transfers between devices  38.7 us (21%)
  between operations  15 us (8%)
  other arithmetic  12.5 us (7%)
  matrix products  5.85 us (3%)
    ppermute x3, waiting for transfers between devices, extended_2(): lax.ppermute(lax.slice_in_dim(block, block.shape[dim] - width, None, axis...  28.1 us
    all_gather x1, waiting for transfers between devices, broadcast(): return lax.all_gather(mine, axis, axis=0, tiled=True)  20.3 us
    ppermute x3, starting transfers between devices, extended_2(): lax.ppermute(lax.slice_in_dim(block, 0, width, axis=dim), axis, backward)  16 us
    ppermute x4, starting transfers between devices, doubling_sum(): lax.ppermute(array, axis, [(i, i ^ step) for i in range(count)])  13.1 us
    slice x8, local copies, waits for them, and re-layouts, lap_periodic(): jnp.roll(grid_field, -2, which_axis)  11.6 us
    ppermute x4, waiting for transfers between devices, doubling_sum(): lax.ppermute(array, axis, [(i, i ^ step) for i in range(count)])  11.1 us
    slice x8, local copies, waits for them, and re-layouts, lap_periodic(): jnp.roll(grid_field, -1, which_axis)  9.01 us
    ppermute x3, waiting for transfers between devices, extended_2(): lax.ppermute(lax.slice_in_dim(block, 0, width, axis=dim), axis, backward)  8.4 us
  transfers between devices with their start and end apart: 12, of which 12 were waited for; matrix products, arithmetic and copies ran while one was open for 21% of the time, Pallas kernels for 0%

profile of v1, /device:TPU:0, one launch (start us, length us, event | category | flops | bytes accessed | tf_op | source)
XLA Modules:
  0.0 180.9 jit_solution(8755249420337557614)
XLA Ops:
  7.2 2.4 %fusion.87 = (f32[64,2,8,128]{3,2,1,0:T(8,128)}, f32[64,2,8,128]{3,2,1,0:T(8,128)}) fusion(f32[64,4,8,128]{3,2,1,0:T(8,128)} %param.3), kind=kLoop, calls=%fused_computation.125 | loop fusion | bytes 2097152 | tf_op jit(solution)/shard_map/slice | solution.py:17
  9.5 1.5 collective-permute-start
  11.0 5.3 %collective-permute-start.1 = (f32[64,2,8,128]{3,2,1,0:T(8,128)}, f32[64,2,8,128]{3,2,1,0:T(8,128)}, u32[]{:S(2)}, u32[]{:S(2)}) collective-permute-start(f32[64,2,8,128]{3,2,1,0:T(8,128)} %get-tuple-element.47), channel_id=1, source_target_pairs={{1,0},{2,1},{3,2},{4,3},{5,4},{6,5},{7,6},{8,7},{9,8},{10,9},{11,1... | collective-permute-start | bytes 1572872 | tf_op jit(solution)/shard_map/ppermute | solution.py:19
  16.6 1.6 fusion.91
  18.2 1.7 fusion.92
  20.0 1.7 fusion.93
  21.7 1.7 fusion.94
  23.4 1.7 fusion.95
  25.1 0.9 fusion.88
  25.9 0.8 fusion.90
  27.4 6.3 %collective-permute-done = f32[64,2,8,128]{3,2,1,0:T(8,128)} collective-permute-done((f32[64,2,8,128]{3,2,1,0:T(8,128)}, f32[64,2,8,128]{3,2,1,0:T(8,128)}, u32[]{:S(2)}, u32[]{:S(2)}) %collective-permute-start) | collective-permute-done | bytes 524320 | tf_op jit(solution)/shard_map/ppermute | solution.py:16
  33.8 1.2 constant_dynamic-update-slice_fusion.1
  35.1 2.4 %collective-permute-done.1 = f32[64,2,8,128]{3,2,1,0:T(8,128)} collective-permute-done((f32[64,2,8,128]{3,2,1,0:T(8,128)}, f32[64,2,8,128]{3,2,1,0:T(8,128)}, u32[]{:S(2)}, u32[]{:S(2)}) %collective-permute-start.1) | collective-permute-done | bytes 524320 | tf_op jit(solution)/shard_map/ppermute | solution.py:19
  37.5 1.1 constant_dynamic-update-slice_fusion.2
  38.6 4.4 %broadcast_multiply_fusion = (f32[64,4,8,128]{3,2,1,0:T(8,128)S(1)}, f32[64,4,8,128]{3,2,1,0:T(8,128)S(1)}) fusion(f32[64,4,8,128]{3,2,1,0:T(8,128)S(1)} %copy-done, f32[4,8,128]{2,1,0:T(8,128)S(1)} %copy-done.11, f32[64,4,8,1]{3,2,1,0:T(8,128)} %get-tuple-element.61, f32[64,4,8,127]{3,2,1,0:T(8,128)} %get-tuple-element.63, ...), kind=kLoop, calls=%fused_computation.96 | loop fusion | flops 9175040 | bytes 15745024 | tf_op jit(solution)/shard_map/div | solution.py:59
  45.1 2.7 %collective-permute-start.2 = (f32[64,2,8,128]{3,2,1,0:T(8,128)S(1)}, f32[64,2,8,128]{3,2,1,0:T(8,128)S(1)}, u32[]{:S(2)}, u32[]{:S(2)}) collective-permute-start(f32[64,2,8,128]{3,2,1,0:T(8,128)S(1)} %get-tuple-element.42), channel_id=1, source_target_pairs={{0,1},{1,2},{2,3},{3,4},{4,5},{5,6},{6,7},{7,8},{8,9},{9,10},{10,1... | collective-permute-start | bytes 1572872 | tf_op jit(solution)/shard_map/ppermute | solution.py:16
  47.8 5.4 %collective-permute-start.3 = (f32[64,2,8,128]{3,2,1,0:T(8,128)S(1)}, f32[64,2,8,128]{3,2,1,0:T(8,128)S(1)}, u32[]{:S(2)}, u32[]{:S(2)}) collective-permute-start(f32[64,2,8,128]{3,2,1,0:T(8,128)S(1)} %get-tuple-element.43), channel_id=1, source_target_pairs={{1,0},{2,1},{3,2},{4,3},{5,4},{6,5},{7,6},{8,7},{9,8},{10,9},{11,1... | collective-permute-start | bytes 1572872 | tf_op jit(solution)/shard_map/ppermute | solution.py:19
  53.7 15.7 %collective-permute-done.2 = f32[64,2,8,128]{3,2,1,0:T(8,128)S(1)} collective-permute-done((f32[64,2,8,128]{3,2,1,0:T(8,128)S(1)}, f32[64,2,8,128]{3,2,1,0:T(8,128)S(1)}, u32[]{:S(2)}, u32[]{:S(2)}) %collective-permute-start.2) | collective-permute-done | bytes 524320 | tf_op jit(solution)/shard_map/ppermute | solution.py:16
  69.4 3.7 %collective-permute-done.3 = f32[64,2,8,128]{3,2,1,0:T(8,128)S(1)} collective-permute-done((f32[64,2,8,128]{3,2,1,0:T(8,128)S(1)}, f32[64,2,8,128]{3,2,1,0:T(8,128)S(1)}, u32[]{:S(2)}, u32[]{:S(2)}) %collective-permute-start.3) | collective-permute-done | bytes 524320 | tf_op jit(solution)/shard_map/ppermute | solution.py:19
  73.1 3.4 %fusion.25 = f32[64,4,8,128]{3,2,1,0:T(8,128)} fusion(f32[64,4,8,128]{3,2,1,0:T(8,128)S(1)} %copy-done, f32[64,4,8,128]{3,2,1,0:T(8,128)S(1)} %get-tuple-element.6, f32[64,2,8,128]{3,2,1,0:T(8,128)S(1)} %collective-permute-done.3, f32[64,2,8,128]{3,2,1,0:T(8,128)S(1)} %collective-permute-done.2, f32[64,4,6,128]{3,2,1,0:T(8,128)S(1)} %get-tuple-element.39, ...), kind=kLoop, calls=%fused_computation.35 | loop fusion | flops 10485760 | bytes 13647872 | tf_op jit(solution)/shard_map/sub | solution.py:69
  76.5 4.5 %all-to-all-start = ((f32[64,4,8,128]{3,2,1,0:T(8,128)}), f32[64,4,8,128]{3,2,1,0:T(8,128)S(1)}, u32[]{:S(2)}, u32[]{:S(2)}) async-start(f32[64,4,8,128]{3,2,1,0:T(8,128)} %fusion.25), calls=%async_computation | async-start | bytes 2097152 | tf_op jit(solution)/shard_map/all_to_all | solution.py:27
  81.1 2.3 %fusion.77 = (f32[64,2,8,128]{3,2,1,0:T(8,128)}, f32[64,2,8,128]{3,2,1,0:T(8,128)}) fusion(f32[64,4,8,128]{3,2,1,0:T(8,128)} %fusion.25), kind=kLoop, calls=%fused_computation.115 | loop fusion | bytes 2097152 | tf_op jit(solution)/shard_map/slice | solution.py:17
  83.3 0.9 collective-permute-start.4
  84.2 5.3 %collective-permute-start.5 = (f32[64,2,8,128]{3,2,1,0:T(8,128)}, f32[64,2,8,128]{3,2,1,0:T(8,128)}, u32[]{:S(2)}, u32[]{:S(2)}) collective-permute-start(f32[64,2,8,128]{3,2,1,0:T(8,128)} %get-tuple-element.25), channel_id=1, source_target_pairs={{1,0},{2,1},{3,2},{4,3},{5,4},{6,5},{7,6},{8,7},{9,8},{10,9},{11,1... | collective-permute-start | bytes 1572872 | tf_op jit(solution)/shard_map/ppermute | solution.py:19
  89.5 2.0 %fusion.70 = (f32[64,4,8,1]{3,2,1,0:T(8,128)S(1)}, f32[64,4,8,1]{3,2,1,0:T(8,128)S(1)}) fusion(f32[64,4,8,128]{3,2,1,0:T(8,128)} %fusion.25), kind=kLoop, calls=%fused_computation.108 | loop fusion | bytes 32768 | tf_op jit(solution)/shard_map/jit(_roll_static)/slice | solution.py:43
  91.6 3.3 %fusion.71 = (f32[64,4,8,126]{3,2,1,0:T(8,128)}, f32[64,4,8,126]{3,2,1,0:T(8,128)}) fusion(f32[64,4,8,128]{3,2,1,0:T(8,128)} %fusion.25), kind=kLoop, calls=%fused_computation.109 | loop fusion | bytes 4128768 | tf_op jit(solution)/shard_map/jit(_roll_static)/slice | solution.py:42
  94.9 3.3 %fusion.72 = (f32[64,4,8,2]{3,2,1,0:T(8,128)}, f32[64,4,8,2]{3,2,1,0:T(8,128)}) fusion(f32[64,4,8,128]{3,2,1,0:T(8,128)} %fusion.25), kind=kLoop, calls=%fused_computation.110 | loop fusion | bytes 65536 | tf_op jit(solution)/shard_map/jit(_roll_static)/slice | solution.py:42
  98.2 1.4 all-to-all-done
  99.6 0.7 constant_dynamic-slice_fusion
  100.3 1.9 %fusion.76 = (f32[64,4,2,128]{3,2,1,0:T(2,128)S(1)}, f32[64,4,2,128]{3,2,1,0:T(2,128)S(1)}) fusion(f32[64,4,8,128]{3,2,1,0:T(8,128)} %fusion.25), kind=kLoop, calls=%fused_computation.114 | loop fusion | bytes 1048576 | tf_op jit(solution)/shard_map/jit(_roll_static)/slice | solution.py:42
  102.1 1.9 %fusion.73 = (f32[64,4,7,128]{3,2,1,0:T(8,128)S(1)}, f32[64,4,7,128]{3,2,1,0:T(8,128)S(1)}) fusion(f32[64,4,8,128]{3,2,1,0:T(8,128)} %fusion.25), kind=kLoop, calls=%fused_computation.111 | loop fusion | bytes 3670016 | tf_op jit(solution)/shard_map/jit(_roll_static)/slice | solution.py:43
  104.0 1.9 %fusion.75 = (f32[64,4,6,128]{3,2,1,0:T(8,128)S(1)}, f32[64,4,6,128]{3,2,1,0:T(8,128)S(1)}) fusion(f32[64,4,8,128]{3,2,1,0:T(8,128)} %fusion.25), kind=kLoop, calls=%fused_computation.113 | loop fusion | bytes 3145728 | tf_op jit(solution)/shard_map/jit(_roll_static)/slice | solution.py:42
  105.9 1.9 %fusion.74 = (f32[64,4,1,128]{3,2,1,0:T(1,128)S(1)}, f32[64,4,1,128]{3,2,1,0:T(1,128)S(1)}) fusion(f32[64,4,8,128]{3,2,1,0:T(8,128)} %fusion.25), kind=kLoop, calls=%fused_computation.112 | loop fusion | bytes 524288 | tf_op jit(solution)/shard_map/jit(_roll_static)/slice | solution.py:43
  107.8 2.1 %fusion.69 = (f32[64,4,8,127]{3,2,1,0:T(8,128)S(1)}, f32[64,4,8,127]{3,2,1,0:T(8,128)S(1)}) fusion(f32[64,4,8,128]{3,2,1,0:T(8,128)} %fusion.25), kind=kLoop, calls=%fused_computation.107 | loop fusion | bytes 4161536 | tf_op jit(solution)/shard_map/jit(_roll_static)/slice | solution.py:43
  109.9 6.1 %collective-permute-done.4 = f32[64,2,8,128]{3,2,1,0:T(8,128)} collective-permute-done((f32[64,2,8,128]{3,2,1,0:T(8,128)}, f32[64,2,8,128]{3,2,1,0:T(8,128)}, u32[]{:S(2)}, u32[]{:S(2)}) %collective-permute-start.4) | collective-permute-done | bytes 524320 | tf_op jit(solution)/shard_map/ppermute | solution.py:16
  116.0 2.3 %collective-permute-done.5 = f32[64,2,8,128]{3,2,1,0:T(8,128)} collective-permute-done((f32[64,2,8,128]{3,2,1,0:T(8,128)}, f32[64,2,8,128]{3,2,1,0:T(8,128)}, u32[]{:S(2)}, u32[]{:S(2)}) %collective-permute-start.5) | collective-permute-done | bytes 524320 | tf_op jit(solution)/shard_map/ppermute | solution.py:19
  118.3 4.6 %fusion.12 = f32[64,4,8,128]{3,2,1,0:T(8,128)S(1)} fusion(f32[64,4,8,128]{3,2,1,0:T(8,128)} %fusion.25, f32[64,2,8,128]{3,2,1,0:T(8,128)} %collective-permute-done.5, f32[64,2,8,128]{3,2,1,0:T(8,128)} %collective-permute-done.4, f32[64,4,6,128]{3,2,1,0:T(8,128)S(1)} %get-tuple-element.21, f32[64,4,2,128]{3,2,1,0:T(2,128)S(1)} %get-tuple-element.23, ...), kind=kLoop, calls=%fused_computation.22 | loop fusion | flops 9437184 | bytes 11550720 | tf_op jit(solution)/shard_map/add | solution.py:55
  122.9 20.3 %all-gather.2.cloned.1.call-done = f32[64,4,8,128]{3,2,1,0:T(8,128)} async-done(((f32[4,4,8,128]{3,2,1,0:T(8,128)}), f32[64,4,8,128]{3,2,1,0:T(8,128)}) %all-gather.2.cloned.1.call-update) | async-done | bytes 1048592 | tf_op jit(solution)/shard_map/all_gather | solution.py:29
  143.2 3.7 %fusion.3 = f32[1,64,64]{2,1,0:T(8,128)S(1)} fusion(f32[64,4,8,128]{3,2,1,0:T(8,128)} %fusion.25, f32[64,4,8,128]{3,2,1,0:T(8,128)} %all-gather.2.cloned.1.call-done), kind=kOutput, calls=%fused_computation.13 | convolution fusion | flops 201330688 | bytes 2113536 | tf_op jit(solution)/shard_map/pc,bc->pb/dot_general | solution.py:82
  147.0 2.1 %fusion.1 = f32[1,64,64]{2,1,0:T(8,128)S(1)} fusion(f32[64,4,8,128]{3,2,1,0:T(8,128)S(1)} %fusion.12, f32[64,4,8,128]{3,2,1,0:T(8,128)S(1)} %copy-done.6), kind=kOutput, calls=%fused_computation.10 | convolution fusion | flops 201330688 | bytes 2113536 | tf_op jit(solution)/shard_map/pc,bc->pb/dot_general | solution.py:79
  149.1 2.6 %collective-permute-start.6 = (f32[2,64,64]{2,1,0:T(8,128)S(1)}, f32[2,64,64]{2,1,0:T(8,128)S(1)}, u32[]{:S(2)}, u32[]{:S(2)}) collective-permute-start(f32[2,64,64]{2,1,0:T(8,128)S(1)} %pad_maximum_fusion.4), channel_id=1, source_target_pairs={{0,1},{1,0},{2,3},{3,2},{4,5},{5,4},{6,7},{7,6},{8,9},{9,8},{10,11... | collective-permute-start | bytes 98312 | tf_op jit(solution)/shard_map/ppermute | solution.py:36
  151.8 3.2 %collective-permute-done.6 = f32[2,64,64]{2,1,0:T(8,128)S(1)} collective-permute-done((f32[2,64,64]{2,1,0:T(8,128)S(1)}, f32[2,64,64]{2,1,0:T(8,128)S(1)}, u32[]{:S(2)}, u32[]{:S(2)}) %collective-permute-start.6) | collective-permute-done | bytes 32800 | tf_op jit(solution)/shard_map/ppermute | solution.py:36
  155.0 1.5 collective-permute-start.7
  156.5 2.8 %collective-permute-done.7 = f32[2,64,64]{2,1,0:T(8,128)S(1)} collective-permute-done((f32[2,64,64]{2,1,0:T(8,128)S(1)}, f32[2,64,64]{2,1,0:T(8,128)S(1)}, u32[]{:S(2)}, u32[]{:S(2)}) %collective-permute-start.7) | collective-permute-done | bytes 32800 | tf_op jit(solution)/shard_map/ppermute | solution.py:36
  159.4 2.5 %collective-permute-start.8 = (f32[2,64,64]{2,1,0:T(8,128)S(1)}, f32[2,64,64]{2,1,0:T(8,128)S(1)}, u32[]{:S(2)}, u32[]{:S(2)}) collective-permute-start(f32[2,64,64]{2,1,0:T(8,128)S(1)} %fusion.96), channel_id=1, source_target_pairs={{0,4},{1,5},{2,6},{3,7},{4,0},{5,1},{6,2},{7,3},{8,12},{9,13},{10,... | collective-permute-start | bytes 98312 | tf_op jit(solution)/shard_map/ppermute | solution.py:36
  161.9 2.7 %collective-permute-done.8 = f32[2,64,64]{2,1,0:T(8,128)S(1)} collective-permute-done((f32[2,64,64]{2,1,0:T(8,128)S(1)}, f32[2,64,64]{2,1,0:T(8,128)S(1)}, u32[]{:S(2)}, u32[]{:S(2)}) %collective-permute-start.8) | collective-permute-done | bytes 32800 | tf_op jit(solution)/shard_map/ppermute | solution.py:36
  164.6 6.4 %collective-permute-start.9 = (f32[2,64,64]{2,1,0:T(8,128)S(1)}, f32[2,64,64]{2,1,0:T(8,128)S(1)}, u32[]{:S(2)}, u32[]{:S(2)}) collective-permute-start(f32[2,64,64]{2,1,0:T(8,128)S(1)} %add.162), channel_id=1, source_target_pairs={{0,8},{1,9},{2,10},{3,11},{4,12},{5,13},{6,14},{7,15},{8,0},{9,1},... | collective-permute-start | bytes 98312 | tf_op jit(solution)/shard_map/ppermute | solution.py:36
  171.0 2.3 %collective-permute-done.9 = f32[2,64,64]{2,1,0:T(8,128)S(1)} collective-permute-done((f32[2,64,64]{2,1,0:T(8,128)S(1)}, f32[2,64,64]{2,1,0:T(8,128)S(1)}, u32[]{:S(2)}, u32[]{:S(2)}) %collective-permute-start.9) | collective-permute-done | bytes 32800 | tf_op jit(solution)/shard_map/ppermute | solution.py:36
  (44 shorter events, 3.7 us)
Async XLA Ops:
  7.2 9.2 %copy-start = (f32[64,4,8,128]{3,2,1,0:T(8,128)S(1)}, f32[64,4,8,128]{3,2,1,0:T(8,128)}, u32[]{:S(2)}) copy-start(f32[64,4,8,128]{3,2,1,0:T(8,128)} %param.3) | copy-start | bytes 3145732
  9.5 24.2 %collective-permute-start = (f32[64,2,8,128]{3,2,1,0:T(8,128)}, f32[64,2,8,128]{3,2,1,0:T(8,128)}, u32[]{:S(2)}, u32[]{:S(2)}) collective-permute-start(f32[64,2,8,128]{3,2,1,0:T(8,128)} %get-tuple-element.46), channel_id=1, source_target_pairs={{0,1},{1,2},{2,3},{3,4},{4,5},{5,6},{6,7},{7,8},{8,9},{9,10},{10,1... | collective-permute-start | bytes 1572872 | tf_op jit(solution)/shard_map/ppermute | solution.py:16
  11.0 26.4 %collective-permute-start.1 = (f32[64,2,8,128]{3,2,1,0:T(8,128)}, f32[64,2,8,128]{3,2,1,0:T(8,128)}, u32[]{:S(2)}, u32[]{:S(2)}) collective-permute-start(f32[64,2,8,128]{3,2,1,0:T(8,128)} %get-tuple-element.47), channel_id=1, source_target_pairs={{1,0},{2,1},{3,2},{4,3},{5,4},{6,5},{7,6},{8,7},{9,8},{10,9},{11,1... | collective-permute-start | bytes 1572872 | tf_op jit(solution)/shard_map/ppermute | solution.py:19
  25.1 2.3 %copy-start.11 = (f32[4,8,128]{2,1,0:T(8,128)S(1)}, f32[4,8,128]{2,1,0:T(8,128)}, u32[]{:S(2)}) copy-start(f32[4,8,128]{2,1,0:T(8,128)} %param.4) | copy-start | bytes 49156
  33.8 4.8 %copy-start.5 = (f32[64,4,8,126]{3,2,1,0:T(8,128)S(1)}, f32[64,4,8,126]{3,2,1,0:T(8,128)}, u32[]{:S(2)}) copy-start(f32[64,4,8,126]{3,2,1,0:T(8,128)} %get-tuple-element.58) | copy-start | bytes 3096580
  34.9 3.6 %copy-start.1 = (f32[64,4,7,128]{3,2,1,0:T(8,128)S(1)}, f32[64,4,7,128]{3,2,1,0:T(8,128)}, u32[]{:S(2)}) copy-start(f32[64,4,7,128]{3,2,1,0:T(8,128)} %get-tuple-element.54) | copy-start | bytes 2752516
  34.9 3.6 %copy-start.2 = (f32[64,4,7,128]{3,2,1,0:T(8,128)S(1)}, f32[64,4,7,128]{3,2,1,0:T(8,128)}, u32[]{:S(2)}) copy-start(f32[64,4,7,128]{3,2,1,0:T(8,128)} %get-tuple-element.55) | copy-start | bytes 2752516
  34.9 3.6 %copy-start.3 = (f32[64,4,8,2]{3,2,1,0:T(8,128)S(1)}, f32[64,4,8,2]{3,2,1,0:T(8,128)}, u32[]{:S(2)}) copy-start(f32[64,4,8,2]{3,2,1,0:T(8,128)} %get-tuple-element.56) | copy-start | bytes 49156
  35.0 3.6 %copy-start.4 = (f32[64,4,8,2]{3,2,1,0:T(8,128)S(1)}, f32[64,4,8,2]{3,2,1,0:T(8,128)}, u32[]{:S(2)}) copy-start(f32[64,4,8,2]{3,2,1,0:T(8,128)} %get-tuple-element.57) | copy-start | bytes 49156
  45.1 24.3 %collective-permute-start.2 = (f32[64,2,8,128]{3,2,1,0:T(8,128)S(1)}, f32[64,2,8,128]{3,2,1,0:T(8,128)S(1)}, u32[]{:S(2)}, u32[]{:S(2)}) collective-permute-start(f32[64,2,8,128]{3,2,1,0:T(8,128)S(1)} %get-tuple-element.42), channel_id=1, source_target_pairs={{0,1},{1,2},{2,3},{3,4},{4,5},{5,6},{6,7},{7,8},{8,9},{9,10},{10,1... | collective-permute-start | bytes 1572872 | tf_op jit(solution)/shard_map/ppermute | solution.py:16
  47.8 25.3 %collective-permute-start.3 = (f32[64,2,8,128]{3,2,1,0:T(8,128)S(1)}, f32[64,2,8,128]{3,2,1,0:T(8,128)S(1)}, u32[]{:S(2)}, u32[]{:S(2)}) collective-permute-start(f32[64,2,8,128]{3,2,1,0:T(8,128)S(1)} %get-tuple-element.43), channel_id=1, source_target_pairs={{1,0},{2,1},{3,2},{4,3},{5,4},{6,5},{7,6},{8,7},{9,8},{10,9},{11,1... | collective-permute-start | bytes 1572872 | tf_op jit(solution)/shard_map/ppermute | solution.py:19
  76.5 23.1 %all-to-all-start = ((f32[64,4,8,128]{3,2,1,0:T(8,128)}), f32[64,4,8,128]{3,2,1,0:T(8,128)S(1)}, u32[]{:S(2)}, u32[]{:S(2)}) async-start(f32[64,4,8,128]{3,2,1,0:T(8,128)} %fusion.25), calls=%async_computation | async-start | bytes 2097152 | tf_op jit(solution)/shard_map/all_to_all | solution.py:27
  81.0 62.2 %all-gather.2.cloned.1.call-start = ((), (), s32[]{:S(2)}) async-start(), calls=%async_computation.1 | async-start | bytes 1114112 | tf_op jit(solution)/shard_map/all_gather | solution.py:29
  83.3 32.6 %collective-permute-start.4 = (f32[64,2,8,128]{3,2,1,0:T(8,128)}, f32[64,2,8,128]{3,2,1,0:T(8,128)}, u32[]{:S(2)}, u32[]{:S(2)}) collective-permute-start(f32[64,2,8,128]{3,2,1,0:T(8,128)} %get-tuple-element.24), channel_id=1, source_target_pairs={{0,1},{1,2},{2,3},{3,4},{4,5},{5,6},{6,7},{7,8},{8,9},{9,10},{10,1... | collective-permute-start | bytes 1572872 | tf_op jit(solution)/shard_map/ppermute | solution.py:16
  84.2 34.1 %collective-permute-start.5 = (f32[64,2,8,128]{3,2,1,0:T(8,128)}, f32[64,2,8,128]{3,2,1,0:T(8,128)}, u32[]{:S(2)}, u32[]{:S(2)}) collective-permute-start(f32[64,2,8,128]{3,2,1,0:T(8,128)} %get-tuple-element.25), channel_id=1, source_target_pairs={{1,0},{2,1},{3,2},{4,3},{5,4},{6,5},{7,6},{8,7},{9,8},{10,9},{11,1... | collective-permute-start | bytes 1572872 | tf_op jit(solution)/shard_map/ppermute | solution.py:19
  107.8 10.5 %copy-start.7 = (f32[64,4,8,126]{3,2,1,0:T(8,128)S(1)}, f32[64,4,8,126]{3,2,1,0:T(8,128)}, u32[]{:S(2)}) copy-start(f32[64,4,8,126]{3,2,1,0:T(8,128)} %get-tuple-element.12) | copy-start | bytes 3096580
  107.8 10.5 %copy-start.8 = (f32[64,4,8,126]{3,2,1,0:T(8,128)S(1)}, f32[64,4,8,126]{3,2,1,0:T(8,128)}, u32[]{:S(2)}) copy-start(f32[64,4,8,126]{3,2,1,0:T(8,128)} %get-tuple-element.13) | copy-start | bytes 3096580
  107.8 10.5 %copy-start.9 = (f32[64,4,8,2]{3,2,1,0:T(8,128)S(1)}, f32[64,4,8,2]{3,2,1,0:T(8,128)}, u32[]{:S(2)}) copy-start(f32[64,4,8,2]{3,2,1,0:T(8,128)} %get-tuple-element.14) | copy-start | bytes 49156
  107.8 10.5 %copy-start.10 = (f32[64,4,8,2]{3,2,1,0:T(8,128)S(1)}, f32[64,4,8,2]{3,2,1,0:T(8,128)}, u32[]{:S(2)}) copy-start(f32[64,4,8,2]{3,2,1,0:T(8,128)} %get-tuple-element.15) | copy-start | bytes 49156
  143.2 3.7 %copy-start.6 = (f32[64,4,8,128]{3,2,1,0:T(8,128)S(1)}, f32[64,4,8,128]{3,2,1,0:T(8,128)}, u32[]{:S(2)}) copy-start(f32[64,4,8,128]{3,2,1,0:T(8,128)} %all-gather.2.cloned.1.call-done) | copy-start | bytes 3145732
  149.1 5.9 %collective-permute-start.6 = (f32[2,64,64]{2,1,0:T(8,128)S(1)}, f32[2,64,64]{2,1,0:T(8,128)S(1)}, u32[]{:S(2)}, u32[]{:S(2)}) collective-permute-start(f32[2,64,64]{2,1,0:T(8,128)S(1)} %pad_maximum_fusion.4), channel_id=1, source_target_pairs={{0,1},{1,0},{2,3},{3,2},{4,5},{5,4},{6,7},{7,6},{8,9},{9,8},{10,11... | collective-permute-start | bytes 98312 | tf_op jit(solution)/shard_map/ppermute | solution.py:36
  155.0 4.4 %collective-permute-start.7 = (f32[2,64,64]{2,1,0:T(8,128)S(1)}, f32[2,64,64]{2,1,0:T(8,128)S(1)}, u32[]{:S(2)}, u32[]{:S(2)}) collective-permute-start(f32[2,64,64]{2,1,0:T(8,128)S(1)} %fusion.67), channel_id=1, source_target_pairs={{0,2},{1,3},{2,0},{3,1},{4,6},{5,7},{6,4},{7,5},{8,10},{9,11},{10,... | collective-permute-start | bytes 98312 | tf_op jit(solution)/shard_map/ppermute | solution.py:36
  159.4 5.3 %collective-permute-start.8 = (f32[2,64,64]{2,1,0:T(8,128)S(1)}, f32[2,64,64]{2,1,0:T(8,128)S(1)}, u32[]{:S(2)}, u32[]{:S(2)}) collective-permute-start(f32[2,64,64]{2,1,0:T(8,128)S(1)} %fusion.96), channel_id=1, source_target_pairs={{0,4},{1,5},{2,6},{3,7},{4,0},{5,1},{6,2},{7,3},{8,12},{9,13},{10,... | collective-permute-start | bytes 98312 | tf_op jit(solution)/shard_map/ppermute | solution.py:36
  164.6 8.8 %collective-permute-start.9 = (f32[2,64,64]{2,1,0:T(8,128)S(1)}, f32[2,64,64]{2,1,0:T(8,128)S(1)}, u32[]{:S(2)}, u32[]{:S(2)}) collective-permute-start(f32[2,64,64]{2,1,0:T(8,128)S(1)} %add.162), channel_id=1, source_target_pairs={{0,8},{1,9},{2,10},{3,11},{4,12},{5,13},{6,14},{7,15},{8,0},{9,1},... | collective-permute-start | bytes 98312 | tf_op jit(solution)/shard_map/ppermute | solution.py:36
Sparse Core Ops, SparseCore 0:
  100.4 42.8 all-gather.1

commit v2 on v1

--- a/solution.py
+++ b/solution.py
@@ -26,7 +26,7 @@
     piece = array.shape[0] // count
     spread = lax.all_to_all(array, axis, 0, 0, tiled=True)
     mine = lax.dynamic_slice_in_dim(spread, root * piece, piece, 0)
-    return lax.all_gather(mine, axis, axis=0, tiled=True)
+    return lax.all_to_all(jnp.concatenate([mine] * count, 0), axis, 0, 0, tiled=True)
 
 
 def doubling_sum(array, axis):

time: 183 us -> 166 us (0.907)
  waiting for transfers between devices: 69.4 us -> 50.8 us
  local copies, waits for them, and re-layouts: 39.4 us -> 53.9 us
  between operations: 15 us -> 1.68 us
    all_gather x1 -> x0, waiting for transfers between devices: 20.3 us -> none  [broadcast(): return lax.all_gather(mine, axis, axis=0, tiled=True)]
    unnamed x25 -> x44, local copies, waits for them, and re-layouts: 1.21 us -> 11.5 us
    ppermute x3, waiting for transfers between devices: 28.1 us -> 22.1 us  [extended_2(): lax.ppermute(lax.slice_in_dim(block, block.shape[dim] - width, None, axis...]
    all_to_all x0 -> x1, waiting for transfers between devices: none -> 5.83 us  [broadcast(): lax.all_to_all(jnp.concatenate([mine] * count, 0), axis, 0, 0, tiled=True)]
    ppermute x4, waiting for transfers between devices: 11.1 us -> 16.9 us  [doubling_sum(): lax.ppermute(array, axis, [(i, i ^ step) for i in range(count)])]
    all_to_all x0 -> x1, starting transfers between devices: none -> 5.17 us  [broadcast(): lax.all_to_all(jnp.concatenate([mine] * count, 0), axis, 0, 0, tiled=True)]
    ppermute x4, starting transfers between devices: 13.1 us -> 8.45 us  [doubling_sum(): lax.ppermute(array, axis, [(i, i ^ step) for i in range(count)])]
    ppermute x3, waiting for transfers between devices: 8.4 us -> 6.06 us  [extended_2(): lax.ppermute(lax.slice_in_dim(block, 0, width, axis=dim), axis, backward)]
  transfers between devices with their start and end apart: 12 -> 12, of which waited for: 12 -> 9; matrix products, arithmetic and copies ran while one was open for 21% -> 32% of each run, Pallas kernels for 0% -> 0%
where the time goes in v2:
time: 166 us; the launch traced here: 165 us
  local copies, waits for them, and re-layouts  53.9 us (32%)
  waiting for transfers between devices  50.8 us (31%)
  starting transfers between devices  39.2 us (24%)
  other arithmetic  13.5 us (8%)
  matrix products  5.47 us (3%)
  between operations  1.68 us (1%)
    ppermute x3, waiting for transfers between devices, extended_2(): lax.ppermute(lax.slice_in_dim(block, block.shape[dim] - width, None, axis...  22.1 us
    ppermute x4, waiting for transfers between devices, doubling_sum(): lax.ppermute(array, axis, [(i, i ^ step) for i in range(count)])  16.9 us
    ppermute x3, starting transfers between devices, extended_2(): lax.ppermute(lax.slice_in_dim(block, 0, width, axis=dim), axis, backward)  16 us
    slice x8, local copies, waits for them, and re-layouts, lap_periodic(): jnp.roll(grid_field, -2, which_axis)  13.6 us
    unnamed x44, local copies, waits for them, and re-layouts  11.5 us
    slice x8, local copies, waits for them, and re-layouts, lap_periodic(): jnp.roll(grid_field, -1, which_axis)  11.2 us
    ppermute x4, starting transfers between devices, doubling_sum(): lax.ppermute(array, axis, [(i, i ^ step) for i in range(count)])  8.45 us
    ppermute x3, waiting for transfers between devices, extended_2(): lax.ppermute(lax.slice_in_dim(block, 0, width, axis=dim), axis, backward)  6.06 us
  transfers between devices with their start and end apart: 12, of which 9 were waited for; matrix products, arithmetic and copies ran while one was open for 32% of the time, Pallas kernels for 0%

profile of v2, /device:TPU:0, one launch (start us, length us, event | category | flops | bytes accessed | tf_op | source)
XLA Modules:
  0.0 164.6 jit_solution(18073847368790606975)
XLA Ops:
  0.6 2.4 %fusion.87 = (f32[64,2,8,128]{3,2,1,0:T(8,128)}, f32[64,2,8,128]{3,2,1,0:T(8,128)}) fusion(f32[64,4,8,128]{3,2,1,0:T(8,128)} %param.3), kind=kLoop, calls=%fused_computation.140 | loop fusion | bytes 2097152 | tf_op jit(solution)/shard_map/slice | solution.py:17
  3.0 1.5 collective-permute-start
  4.5 5.3 %collective-permute-start.1 = (f32[64,2,8,128]{3,2,1,0:T(8,128)}, f32[64,2,8,128]{3,2,1,0:T(8,128)}, u32[]{:S(2)}, u32[]{:S(2)}) collective-permute-start(f32[64,2,8,128]{3,2,1,0:T(8,128)} %get-tuple-element.47), channel_id=1, source_target_pairs={{1,0},{2,1},{3,2},{4,3},{5,4},{6,5},{7,6},{8,7},{9,8},{10,9},{11,1... | collective-permute-start | bytes 1572872 | tf_op jit(solution)/shard_map/ppermute | solution.py:19
  10.1 1.6 fusion.91
  11.7 1.7 %fusion.92 = (f32[64,4,8,2]{3,2,1,0:T(8,128)}, f32[64,4,8,2]{3,2,1,0:T(8,128)}) fusion(f32[64,4,8,128]{3,2,1,0:T(8,128)S(1)} %copy-done), kind=kLoop, calls=%fused_computation.145 | loop fusion | bytes 65536 | tf_op jit(solution)/shard_map/jit(_roll_static)/slice | solution.py:42
  13.4 1.7 %fusion.93 = (f32[64,4,8,126]{3,2,1,0:T(8,128)}, f32[64,4,8,126]{3,2,1,0:T(8,128)}) fusion(f32[64,4,8,128]{3,2,1,0:T(8,128)S(1)} %copy-done), kind=kLoop, calls=%fused_computation.146 | loop fusion | bytes 4128768 | tf_op jit(solution)/shard_map/jit(_roll_static)/slice | solution.py:42
  15.1 1.7 %fusion.94 = (f32[64,4,8,1]{3,2,1,0:T(8,128)}, f32[64,4,8,1]{3,2,1,0:T(8,128)}) fusion(f32[64,4,8,128]{3,2,1,0:T(8,128)S(1)} %copy-done), kind=kLoop, calls=%fused_computation.147 | loop fusion | bytes 32768 | tf_op jit(solution)/shard_map/jit(_roll_static)/slice | solution.py:43
  16.8 1.7 %fusion.95 = (f32[64,4,8,127]{3,2,1,0:T(8,128)}, f32[64,4,8,127]{3,2,1,0:T(8,128)}) fusion(f32[64,4,8,128]{3,2,1,0:T(8,128)S(1)} %copy-done), kind=kLoop, calls=%fused_computation.148 | loop fusion | bytes 4161536 | tf_op jit(solution)/shard_map/jit(_roll_static)/slice | solution.py:43
  18.5 0.9 fusion.88
  19.4 0.8 fusion.90
  20.9 6.3 %collective-permute-done = f32[64,2,8,128]{3,2,1,0:T(8,128)} collective-permute-done((f32[64,2,8,128]{3,2,1,0:T(8,128)}, f32[64,2,8,128]{3,2,1,0:T(8,128)}, u32[]{:S(2)}, u32[]{:S(2)}) %collective-permute-start) | collective-permute-done | bytes 524320 | tf_op jit(solution)/shard_map/ppermute | solution.py:16
  27.2 1.2 constant_dynamic-update-slice_fusion.1
  28.6 2.4 %collective-permute-done.1 = f32[64,2,8,128]{3,2,1,0:T(8,128)} collective-permute-done((f32[64,2,8,128]{3,2,1,0:T(8,128)}, f32[64,2,8,128]{3,2,1,0:T(8,128)}, u32[]{:S(2)}, u32[]{:S(2)}) %collective-permute-start.1) | collective-permute-done | bytes 524320 | tf_op jit(solution)/shard_map/ppermute | solution.py:19
  30.9 1.1 constant_dynamic-update-slice_fusion.2
  32.1 4.4 %broadcast_multiply_fusion = (f32[64,4,8,128]{3,2,1,0:T(8,128)S(1)}, f32[64,4,8,128]{3,2,1,0:T(8,128)S(1)}) fusion(f32[64,4,8,128]{3,2,1,0:T(8,128)S(1)} %copy-done, f32[4,8,128]{2,1,0:T(8,128)S(1)} %copy-done.13, f32[64,4,8,1]{3,2,1,0:T(8,128)} %get-tuple-element.61, f32[64,4,8,127]{3,2,1,0:T(8,128)} %get-tuple-element.63, ...), kind=kLoop, calls=%fused_computation.96 | loop fusion | flops 9175040 | bytes 15745024 | tf_op jit(solution)/shard_map/div | solution.py:59
  38.6 2.7 %collective-permute-start.2 = (f32[64,2,8,128]{3,2,1,0:T(8,128)S(1)}, f32[64,2,8,128]{3,2,1,0:T(8,128)S(1)}, u32[]{:S(2)}, u32[]{:S(2)}) collective-permute-start(f32[64,2,8,128]{3,2,1,0:T(8,128)S(1)} %get-tuple-element.42), channel_id=1, source_target_pairs={{0,1},{1,2},{2,3},{3,4},{4,5},{5,6},{6,7},{7,8},{8,9},{9,10},{10,1... | collective-permute-start | bytes 1572872 | tf_op jit(solution)/shard_map/ppermute | solution.py:16
  41.3 5.4 %collective-permute-start.3 = (f32[64,2,8,128]{3,2,1,0:T(8,128)S(1)}, f32[64,2,8,128]{3,2,1,0:T(8,128)S(1)}, u32[]{:S(2)}, u32[]{:S(2)}) collective-permute-start(f32[64,2,8,128]{3,2,1,0:T(8,128)S(1)} %get-tuple-element.43), channel_id=1, source_target_pairs={{1,0},{2,1},{3,2},{4,3},{5,4},{6,5},{7,6},{8,7},{9,8},{10,9},{11,1... | collective-permute-start | bytes 1572872 | tf_op jit(solution)/shard_map/ppermute | solution.py:19
  47.1 15.7 %collective-permute-done.2 = f32[64,2,8,128]{3,2,1,0:T(8,128)S(1)} collective-permute-done((f32[64,2,8,128]{3,2,1,0:T(8,128)S(1)}, f32[64,2,8,128]{3,2,1,0:T(8,128)S(1)}, u32[]{:S(2)}, u32[]{:S(2)}) %collective-permute-start.2) | collective-permute-done | bytes 524320 | tf_op jit(solution)/shard_map/ppermute | solution.py:16
  62.9 3.7 %collective-permute-done.3 = f32[64,2,8,128]{3,2,1,0:T(8,128)S(1)} collective-permute-done((f32[64,2,8,128]{3,2,1,0:T(8,128)S(1)}, f32[64,2,8,128]{3,2,1,0:T(8,128)S(1)}, u32[]{:S(2)}, u32[]{:S(2)}) %collective-permute-start.3) | collective-permute-done | bytes 524320 | tf_op jit(solution)/shard_map/ppermute | solution.py:19
  66.6 3.4 %fusion.25 = f32[64,4,8,128]{3,2,1,0:T(8,128)} fusion(f32[64,4,8,128]{3,2,1,0:T(8,128)S(1)} %copy-done, f32[64,4,8,128]{3,2,1,0:T(8,128)S(1)} %get-tuple-element.6, f32[64,2,8,128]{3,2,1,0:T(8,128)S(1)} %collective-permute-done.3, f32[64,2,8,128]{3,2,1,0:T(8,128)S(1)} %collective-permute-done.2, f32[64,4,6,128]{3,2,1,0:T(8,128)S(1)} %get-tuple-element.39, ...), kind=kLoop, calls=%fused_computation.35 | loop fusion | flops 10485760 | bytes 13647872 | tf_op jit(solution)/shard_map/sub | solution.py:69
  70.0 4.5 %all-to-all-start = ((f32[64,4,8,128]{3,2,1,0:T(8,128)}), f32[64,4,8,128]{3,2,1,0:T(8,128)S(1)}, u32[]{:S(2)}, u32[]{:S(2)}) async-start(f32[64,4,8,128]{3,2,1,0:T(8,128)} %fusion.25), calls=%async_computation | async-start | bytes 2097152 | tf_op jit(solution)/shard_map/all_to_all | solution.py:27
  74.5 3.0 %fusion.70 = (f32[64,4,8,1]{3,2,1,0:T(8,128)S(1)}, f32[64,4,8,1]{3,2,1,0:T(8,128)}) fusion(f32[64,4,8,128]{3,2,1,0:T(8,128)} %fusion.25), kind=kLoop, calls=%fused_computation.123 | loop fusion | bytes 32768 | tf_op jit(solution)/shard_map/jit(_roll_static)/slice | solution.py:43
  77.5 3.3 %fusion.71 = (f32[64,4,8,126]{3,2,1,0:T(8,128)}, f32[64,4,8,126]{3,2,1,0:T(8,128)}) fusion(f32[64,4,8,128]{3,2,1,0:T(8,128)} %fusion.25), kind=kLoop, calls=%fused_computation.124 | loop fusion | bytes 4128768 | tf_op jit(solution)/shard_map/jit(_roll_static)/slice | solution.py:42
  80.8 2.2 %fusion.77 = (f32[64,2,8,128]{3,2,1,0:T(8,128)}, f32[64,2,8,128]{3,2,1,0:T(8,128)}) fusion(f32[64,4,8,128]{3,2,1,0:T(8,128)} %fusion.25), kind=kLoop, calls=%fused_computation.130 | loop fusion | bytes 2097152 | tf_op jit(solution)/shard_map/slice | solution.py:17
  83.1 2.6 %fusion.76 = (f32[64,4,2,128]{3,2,1,0:T(2,128)S(1)}, f32[64,4,2,128]{3,2,1,0:T(2,128)}) fusion(f32[64,4,8,128]{3,2,1,0:T(8,128)} %fusion.25), kind=kLoop, calls=%fused_computation.129 | loop fusion | bytes 1048576 | tf_op jit(solution)/shard_map/jit(_roll_static)/slice | solution.py:42
  85.6 0.9 collective-permute-start.4
  86.5 5.3 %collective-permute-start.5 = (f32[64,2,8,128]{3,2,1,0:T(8,128)}, f32[64,2,8,128]{3,2,1,0:T(8,128)S(1)}, u32[]{:S(2)}, u32[]{:S(2)}) collective-permute-start(f32[64,2,8,128]{3,2,1,0:T(8,128)} %get-tuple-element.25), channel_id=1, source_target_pairs={{1,0},{2,1},{3,2},{4,3},{5,4},{6,5},{7,6},{8,7},{9,8},{10,9},{11,1... | collective-permute-start | bytes 1572872 | tf_op jit(solution)/shard_map/ppermute | solution.py:19
  91.8 3.4 %fusion.72 = (f32[64,4,8,2]{3,2,1,0:T(8,128)}, f32[64,4,8,2]{3,2,1,0:T(8,128)}) fusion(f32[64,4,8,128]{3,2,1,0:T(8,128)} %fusion.25), kind=kLoop, calls=%fused_computation.125 | loop fusion | bytes 65536 | tf_op jit(solution)/shard_map/jit(_roll_static)/slice | solution.py:42
  95.2 3.2 %fusion.73 = (f32[64,4,7,128]{3,2,1,0:T(8,128)}, f32[64,4,7,128]{3,2,1,0:T(8,128)}) fusion(f32[64,4,8,128]{3,2,1,0:T(8,128)} %fusion.25), kind=kLoop, calls=%fused_computation.126 | loop fusion | bytes 3670016 | tf_op jit(solution)/shard_map/jit(_roll_static)/slice | solution.py:43
  98.3 3.1 %fusion.75 = (f32[64,4,6,128]{3,2,1,0:T(8,128)}, f32[64,4,6,128]{3,2,1,0:T(8,128)}) fusion(f32[64,4,8,128]{3,2,1,0:T(8,128)} %fusion.25), kind=kLoop, calls=%fused_computation.128 | loop fusion | bytes 3145728 | tf_op jit(solution)/shard_map/jit(_roll_static)/slice | solution.py:42
  101.5 0.6 constant_dynamic-update-slice_fusion.19
  108.3 0.6 constant_dynamic-update-slice_fusion.8
  109.0 0.6 constant_dynamic-update-slice_fusion.7
  111.5 5.2 %all-to-all-start.1 = ((f32[64,4,8,128]{3,2,1,0:T(8,128)}), f32[64,4,8,128]{3,2,1,0:T(8,128)S(1)}, u32[]{:S(2)}, u32[]{:S(2)}) async-start(f32[64,4,8,128]{3,2,1,0:T(8,128)} %constant_dynamic-update-slice_fusion.4), calls=%async_computation.1 | async-start | bytes 2097152 | tf_op jit(solution)/shard_map/all_to_all | solution.py:29
  116.6 1.9 %fusion.74 = (f32[64,4,1,128]{3,2,1,0:T(1,128)S(1)}, f32[64,4,1,128]{3,2,1,0:T(1,128)S(1)}) fusion(f32[64,4,8,128]{3,2,1,0:T(8,128)} %fusion.25), kind=kLoop, calls=%fused_computation.127 | loop fusion | bytes 524288 | tf_op jit(solution)/shard_map/jit(_roll_static)/slice | solution.py:43
  118.5 2.1 %fusion.69 = (f32[64,4,8,127]{3,2,1,0:T(8,128)S(1)}, f32[64,4,8,127]{3,2,1,0:T(8,128)S(1)}) fusion(f32[64,4,8,128]{3,2,1,0:T(8,128)} %fusion.25), kind=kLoop, calls=%fused_computation.122 | loop fusion | bytes 4161536 | tf_op jit(solution)/shard_map/jit(_roll_static)/slice | solution.py:43
  120.7 0.8 copy-done.11
  121.6 5.6 %fusion.12 = f32[64,4,8,128]{3,2,1,0:T(8,128)S(1)} fusion(f32[64,4,8,128]{3,2,1,0:T(8,128)} %fusion.25, f32[64,2,8,128]{3,2,1,0:T(8,128)} %copy-done.12, f32[64,2,8,128]{3,2,1,0:T(8,128)} %copy-done.11, f32[64,4,6,128]{3,2,1,0:T(8,128)} %get-tuple-element.21, f32[64,4,2,128]{3,2,1,0:T(2,128)S(1)} %copy-done.10, f32[64,4,2,128]{3,2,1,0:T(2,128)S(1)} %get-tuple-element.22, ...), kind=kLoop, calls=%fused_computation.22 | loop fusion | flops 9437184 | bytes 11550720 | tf_op jit(solution)/shard_map/add | solution.py:55
  127.2 5.8 %all-to-all-done.1 = f32[64,4,8,128]{3,2,1,0:T(8,128)S(1)} async-done(((f32[64,4,8,128]{3,2,1,0:T(8,128)}), f32[64,4,8,128]{3,2,1,0:T(8,128)S(1)}, u32[]{:S(2)}, u32[]{:S(2)}) %all-to-all-start.1) | async-done | bytes 1048608 | tf_op jit(solution)/shard_map/all_to_all | solution.py:29
  133.1 3.3 %fusion.3 = f32[1,64,64]{2,1,0:T(8,128)S(1)} fusion(f32[64,4,8,128]{3,2,1,0:T(8,128)} %fusion.25, f32[64,4,8,128]{3,2,1,0:T(8,128)S(1)} %all-to-all-done.1), kind=kOutput, calls=%fused_computation.13 | convolution fusion | flops 201330688 | bytes 2113536 | tf_op jit(solution)/shard_map/pc,bc->pb/dot_general | solution.py:82
  136.4 2.1 %fusion.1 = f32[1,64,64]{2,1,0:T(8,128)S(1)} fusion(f32[64,4,8,128]{3,2,1,0:T(8,128)S(1)} %fusion.12, f32[64,4,8,128]{3,2,1,0:T(8,128)S(1)} %all-to-all-done.1), kind=kOutput, calls=%fused_computation.10 | convolution fusion | flops 201330688 | bytes 2113536 | tf_op jit(solution)/shard_map/pc,bc->pb/dot_general | solution.py:79
  138.7 5.8 %collective-permute-done.6 = f32[2,64,64]{2,1,0:T(8,128)S(1)} collective-permute-done((f32[2,64,64]{2,1,0:T(8,128)S(1)}, f32[2,64,64]{2,1,0:T(8,128)S(1)}, u32[]{:S(2)}, u32[]{:S(2)}) %collective-permute-start.6) | collective-permute-done | bytes 32800 | tf_op jit(solution)/shard_map/ppermute | solution.py:36
  144.5 4.3 %collective-permute-done.7 = f32[2,64,64]{2,1,0:T(8,128)S(1)} collective-permute-done((f32[2,64,64]{2,1,0:T(8,128)S(1)}, f32[2,64,64]{2,1,0:T(8,128)S(1)}, u32[]{:S(2)}, u32[]{:S(2)}) %collective-permute-start.7) | collective-permute-done | bytes 32800 | tf_op jit(solution)/shard_map/ppermute | solution.py:36
  148.8 0.8 collective-permute-start.8
  149.6 4.6 %collective-permute-done.8 = f32[2,64,64]{2,1,0:T(8,128)S(1)} collective-permute-done((f32[2,64,64]{2,1,0:T(8,128)S(1)}, f32[2,64,64]{2,1,0:T(8,128)S(1)}, u32[]{:S(2)}, u32[]{:S(2)}) %collective-permute-start.8) | collective-permute-done | bytes 32800 | tf_op jit(solution)/shard_map/ppermute | solution.py:36
  154.2 7.5 %collective-permute-start.9 = (f32[2,64,64]{2,1,0:T(8,128)S(1)}, f32[2,64,64]{2,1,0:T(8,128)S(1)}, u32[]{:S(2)}, u32[]{:S(2)}) collective-permute-start(f32[2,64,64]{2,1,0:T(8,128)S(1)} %add.162), channel_id=1, source_target_pairs={{0,8},{1,9},{2,10},{3,11},{4,12},{5,13},{6,14},{7,15},{8,0},{9,1},... | collective-permute-start | bytes 98312 | tf_op jit(solution)/shard_map/ppermute | solution.py:36
  161.7 2.2 %collective-permute-done.9 = f32[2,64,64]{2,1,0:T(8,128)S(1)} collective-permute-done((f32[2,64,64]{2,1,0:T(8,128)S(1)}, f32[2,64,64]{2,1,0:T(8,128)S(1)}, u32[]{:S(2)}, u32[]{:S(2)}) %collective-permute-start.9) | collective-permute-done | bytes 32800 | tf_op jit(solution)/shard_map/ppermute | solution.py:36
  164.0 0.6 slice_bitcast_fusion
  (62 shorter events, 11.4 us)
Async XLA Ops:
  0.6 9.2 %copy-start = (f32[64,4,8,128]{3,2,1,0:T(8,128)S(1)}, f32[64,4,8,128]{3,2,1,0:T(8,128)}, u32[]{:S(2)}) copy-start(f32[64,4,8,128]{3,2,1,0:T(8,128)} %param.3) | copy-start | bytes 3145732
  3.0 24.2 %collective-permute-start = (f32[64,2,8,128]{3,2,1,0:T(8,128)}, f32[64,2,8,128]{3,2,1,0:T(8,128)}, u32[]{:S(2)}, u32[]{:S(2)}) collective-permute-start(f32[64,2,8,128]{3,2,1,0:T(8,128)} %get-tuple-element.46), channel_id=1, source_target_pairs={{0,1},{1,2},{2,3},{3,4},{4,5},{5,6},{6,7},{7,8},{8,9},{9,10},{10,1... | collective-permute-start | bytes 1572872 | tf_op jit(solution)/shard_map/ppermute | solution.py:16
  4.5 26.4 %collective-permute-start.1 = (f32[64,2,8,128]{3,2,1,0:T(8,128)}, f32[64,2,8,128]{3,2,1,0:T(8,128)}, u32[]{:S(2)}, u32[]{:S(2)}) collective-permute-start(f32[64,2,8,128]{3,2,1,0:T(8,128)} %get-tuple-element.47), channel_id=1, source_target_pairs={{1,0},{2,1},{3,2},{4,3},{5,4},{6,5},{7,6},{8,7},{9,8},{10,9},{11,1... | collective-permute-start | bytes 1572872 | tf_op jit(solution)/shard_map/ppermute | solution.py:19
  18.5 2.3 %copy-start.13 = (f32[4,8,128]{2,1,0:T(8,128)S(1)}, f32[4,8,128]{2,1,0:T(8,128)}, u32[]{:S(2)}) copy-start(f32[4,8,128]{2,1,0:T(8,128)} %param.4) | copy-start | bytes 49156
  27.2 4.8 %copy-start.9 = (f32[64,4,8,126]{3,2,1,0:T(8,128)S(1)}, f32[64,4,8,126]{3,2,1,0:T(8,128)}, u32[]{:S(2)}) copy-start(f32[64,4,8,126]{3,2,1,0:T(8,128)} %get-tuple-element.58) | copy-start | bytes 3096580
  28.4 3.6 %copy-start.5 = (f32[64,4,7,128]{3,2,1,0:T(8,128)S(1)}, f32[64,4,7,128]{3,2,1,0:T(8,128)}, u32[]{:S(2)}) copy-start(f32[64,4,7,128]{3,2,1,0:T(8,128)} %get-tuple-element.54) | copy-start | bytes 2752516
  28.4 3.6 %copy-start.6 = (f32[64,4,7,128]{3,2,1,0:T(8,128)S(1)}, f32[64,4,7,128]{3,2,1,0:T(8,128)}, u32[]{:S(2)}) copy-start(f32[64,4,7,128]{3,2,1,0:T(8,128)} %get-tuple-element.55) | copy-start | bytes 2752516
  28.4 3.6 %copy-start.7 = (f32[64,4,8,2]{3,2,1,0:T(8,128)S(1)}, f32[64,4,8,2]{3,2,1,0:T(8,128)}, u32[]{:S(2)}) copy-start(f32[64,4,8,2]{3,2,1,0:T(8,128)} %get-tuple-element.56) | copy-start | bytes 49156
  28.4 3.6 %copy-start.8 = (f32[64,4,8,2]{3,2,1,0:T(8,128)S(1)}, f32[64,4,8,2]{3,2,1,0:T(8,128)}, u32[]{:S(2)}) copy-start(f32[64,4,8,2]{3,2,1,0:T(8,128)} %get-tuple-element.57) | copy-start | bytes 49156
  38.6 24.3 %collective-permute-start.2 = (f32[64,2,8,128]{3,2,1,0:T(8,128)S(1)}, f32[64,2,8,128]{3,2,1,0:T(8,128)S(1)}, u32[]{:S(2)}, u32[]{:S(2)}) collective-permute-start(f32[64,2,8,128]{3,2,1,0:T(8,128)S(1)} %get-tuple-element.42), channel_id=1, source_target_pairs={{0,1},{1,2},{2,3},{3,4},{4,5},{5,6},{6,7},{7,8},{8,9},{9,10},{10,1... | collective-permute-start | bytes 1572872 | tf_op jit(solution)/shard_map/ppermute | solution.py:16
  41.3 25.3 %collective-permute-start.3 = (f32[64,2,8,128]{3,2,1,0:T(8,128)S(1)}, f32[64,2,8,128]{3,2,1,0:T(8,128)S(1)}, u32[]{:S(2)}, u32[]{:S(2)}) collective-permute-start(f32[64,2,8,128]{3,2,1,0:T(8,128)S(1)} %get-tuple-element.43), channel_id=1, source_target_pairs={{1,0},{2,1},{3,2},{4,3},{5,4},{6,5},{7,6},{8,7},{9,8},{10,9},{11,1... | collective-permute-start | bytes 1572872 | tf_op jit(solution)/shard_map/ppermute | solution.py:19
  70.0 31.5 %all-to-all-start = ((f32[64,4,8,128]{3,2,1,0:T(8,128)}), f32[64,4,8,128]{3,2,1,0:T(8,128)S(1)}, u32[]{:S(2)}, u32[]{:S(2)}) async-start(f32[64,4,8,128]{3,2,1,0:T(8,128)} %fusion.25), calls=%async_computation | async-start | bytes 2097152 | tf_op jit(solution)/shard_map/all_to_all | solution.py:27
  85.6 35.0 %collective-permute-start.4 = (f32[64,2,8,128]{3,2,1,0:T(8,128)}, f32[64,2,8,128]{3,2,1,0:T(8,128)S(1)}, u32[]{:S(2)}, u32[]{:S(2)}) collective-permute-start(f32[64,2,8,128]{3,2,1,0:T(8,128)} %get-tuple-element.24), channel_id=1, source_target_pairs={{0,1},{1,2},{2,3},{3,4},{4,5},{5,6},{6,7},{7,8},{8,9},{9,10},{10,1... | collective-permute-start | bytes 1572872 | tf_op jit(solution)/shard_map/ppermute | solution.py:16
  86.5 34.1 %collective-permute-start.5 = (f32[64,2,8,128]{3,2,1,0:T(8,128)}, f32[64,2,8,128]{3,2,1,0:T(8,128)S(1)}, u32[]{:S(2)}, u32[]{:S(2)}) collective-permute-start(f32[64,2,8,128]{3,2,1,0:T(8,128)} %get-tuple-element.25), channel_id=1, source_target_pairs={{1,0},{2,1},{3,2},{4,3},{5,4},{6,5},{7,6},{8,7},{9,8},{10,9},{11,1... | collective-permute-start | bytes 1572872 | tf_op jit(solution)/shard_map/ppermute | solution.py:19
  111.5 21.6 %all-to-all-start.1 = ((f32[64,4,8,128]{3,2,1,0:T(8,128)}), f32[64,4,8,128]{3,2,1,0:T(8,128)S(1)}, u32[]{:S(2)}, u32[]{:S(2)}) async-start(f32[64,4,8,128]{3,2,1,0:T(8,128)} %constant_dynamic-update-slice_fusion.4), calls=%async_computation.1 | async-start | bytes 2097152 | tf_op jit(solution)/shard_map/all_to_all | solution.py:29
  116.6 5.0 %copy-start.10 = (f32[64,4,2,128]{3,2,1,0:T(2,128)S(1)}, f32[64,4,2,128]{3,2,1,0:T(2,128)}, u32[]{:S(2)}) copy-start(f32[64,4,2,128]{3,2,1,0:T(2,128)} %get-tuple-element.23) | copy-start | bytes 786436
  118.5 3.1 %copy-start.1 = (f32[64,4,8,1]{3,2,1,0:T(8,128)S(1)}, f32[64,4,8,1]{3,2,1,0:T(8,128)}, u32[]{:S(2)}) copy-start(f32[64,4,8,1]{3,2,1,0:T(8,128)} %get-tuple-element.11) | copy-start | bytes 24580
  118.5 3.1 %copy-start.2 = (f32[64,4,8,126]{3,2,1,0:T(8,128)S(1)}, f32[64,4,8,126]{3,2,1,0:T(8,128)}, u32[]{:S(2)}) copy-start(f32[64,4,8,126]{3,2,1,0:T(8,128)} %get-tuple-element.12) | copy-start | bytes 3096580
  118.5 3.1 %copy-start.3 = (f32[64,4,8,126]{3,2,1,0:T(8,128)S(1)}, f32[64,4,8,126]{3,2,1,0:T(8,128)}, u32[]{:S(2)}) copy-start(f32[64,4,8,126]{3,2,1,0:T(8,128)} %get-tuple-element.13) | copy-start | bytes 3096580
  118.5 3.1 %copy-start.4 = (f32[64,4,8,2]{3,2,1,0:T(8,128)S(1)}, f32[64,4,8,2]{3,2,1,0:T(8,128)}, u32[]{:S(2)}) copy-start(f32[64,4,8,2]{3,2,1,0:T(8,128)} %get-tuple-element.14) | copy-start | bytes 49156
  120.6 0.8 copy-start.11
  120.6 0.9 copy-start.12
  138.6 5.9 %collective-permute-start.6 = (f32[2,64,64]{2,1,0:T(8,128)S(1)}, f32[2,64,64]{2,1,0:T(8,128)S(1)}, u32[]{:S(2)}, u32[]{:S(2)}) collective-permute-start(f32[2,64,64]{2,1,0:T(8,128)S(1)} %pad_maximum_fusion.4), channel_id=1, source_target_pairs={{0,1},{1,0},{2,3},{3,2},{4,5},{5,4},{6,7},{7,6},{8,9},{9,8},{10,11... | collective-permute-start | bytes 98312 | tf_op jit(solution)/shard_map/ppermute | solution.py:36
  144.4 4.4 %collective-permute-start.7 = (f32[2,64,64]{2,1,0:T(8,128)S(1)}, f32[2,64,64]{2,1,0:T(8,128)S(1)}, u32[]{:S(2)}, u32[]{:S(2)}) collective-permute-start(f32[2,64,64]{2,1,0:T(8,128)S(1)} %fusion.67), channel_id=1, source_target_pairs={{0,2},{1,3},{2,0},{3,1},{4,6},{5,7},{6,4},{7,5},{8,10},{9,11},{10,... | collective-permute-start | bytes 98312 | tf_op jit(solution)/shard_map/ppermute | solution.py:36
  148.8 5.4 %collective-permute-start.8 = (f32[2,64,64]{2,1,0:T(8,128)S(1)}, f32[2,64,64]{2,1,0:T(8,128)S(1)}, u32[]{:S(2)}, u32[]{:S(2)}) collective-permute-start(f32[2,64,64]{2,1,0:T(8,128)S(1)} %fusion.96), channel_id=1, source_target_pairs={{0,4},{1,5},{2,6},{3,7},{4,0},{5,1},{6,2},{7,3},{8,12},{9,13},{10,... | collective-permute-start | bytes 98312 | tf_op jit(solution)/shard_map/ppermute | solution.py:36
  154.2 9.7 %collective-permute-start.9 = (f32[2,64,64]{2,1,0:T(8,128)S(1)}, f32[2,64,64]{2,1,0:T(8,128)S(1)}, u32[]{:S(2)}, u32[]{:S(2)}) collective-permute-start(f32[2,64,64]{2,1,0:T(8,128)S(1)} %add.162), channel_id=1, source_target_pairs={{0,8},{1,9},{2,10},{3,11},{4,12},{5,13},{6,14},{7,15},{8,0},{9,1},... | collective-permute-start | bytes 98312 | tf_op jit(solution)/shard_map/ppermute | solution.py:36

commit v3 on v2

--- a/solution.py
+++ b/solution.py
@@ -5,20 +5,6 @@
 
 center = 4.9
 halfwidth = 4.1
-
-
-def extended_2(block, sides, width):
-    for axis, dim in sides:
-        count = lax.axis_size(axis)
-        forward = [(i, i + 1) for i in range(count - 1)]
-        forward.append((count - 1, 0))
-        backward = [(target, source) for source, target in forward]
-        low = lax.ppermute(
-            lax.slice_in_dim(block, block.shape[dim] - width, None, axis=dim), axis, forward
-        )
-        high = lax.ppermute(lax.slice_in_dim(block, 0, width, axis=dim), axis, backward)
-        block = jnp.concatenate([low, block, high], axis=dim)
-    return block
 
 
 def broadcast(array, axis, root):
@@ -59,14 +45,27 @@
     return (hamiltonian_apply(extended, local_potential) - center * extended[:, 2:-2]) / halfwidth
 
 
-def with_faces(grid_field):
-    return extended_2(grid_field, (("dom", 1),), 2)
+def shifted_to(block, axis, shift):
+    count = lax.axis_size(axis)
+    return lax.ppermute(block, axis, [(i, (i + shift) % count) for i in range(count)])
+
+
+def with_faces(block, dim, axis, width):
+    n = block.shape[dim]
+    low, high = [], []
+    for hop in range(1, -(-width // n) + 1):
+        take = min(n, width - n * (hop - 1))
+        low.insert(0, shifted_to(lax.slice_in_dim(block, n - take, None, axis=dim), axis, hop))
+        high.append(shifted_to(lax.slice_in_dim(block, 0, take, axis=dim), axis, -hop))
+    return jnp.concatenate(low + [block] + high, axis=dim)
 
 
 def body(psi, potential, owner):
-    current = psi
-    first_term = shifted(with_faces(current), potential)
-    current = 2.0 * shifted(with_faces(first_term), potential) - current
+    wide = with_faces(psi, 1, "dom", 6)
+    pot_wide = with_faces(potential, 0, "dom", 4)
+    first_term = shifted(wide, pot_wide)
+    filtered_wide = 2.0 * shifted(first_term, pot_wide[2:-2]) - wide[:, 4:-4]
+    current = filtered_wide[:, 2:-2]
     local_bands = current.shape[0]
     owner_root = owner[0]
     owned_panel = broadcast(current, "band", owner_root)
@@ -74,8 +73,7 @@
     scale = 1.0 / total_cells
     flattened = current.reshape(local_bands, -1)
     panel_flat = owned_panel.reshape(local_bands, -1)
-    extended = extended_2(current, (("dom", 1),), 2)
-    applied = hamiltonian_apply(extended, potential)
+    applied = hamiltonian_apply(filtered_wide, potential)
     ham_rows = jnp.einsum(
         "pc,bc->pb", panel_flat, applied.reshape(local_bands, -1), precision=lax.Precision.HIGHEST
     )

time: 166 us -> 207 us (1.25)
  waiting for transfers between devices: 50.8 us -> 69 us
  local copies, waits for them, and re-layouts: 53.9 us -> 68 us
  other arithmetic: 13.5 us -> 22.5 us
  starting transfers between devices: 39.2 us -> 36.2 us
  matrix products: 5.47 us -> 7.66 us
    slice x11 -> x3, local copies, waits for them, and re-layouts: 15.1 us -> 2.17 us  [the longest x1 2.09 us: with_faces(): lax.slice_in_dim(block, n - take, None, axis=dim)]
    slice x8 -> x12, local copies, waits for them, and re-layouts: 11.2 us -> 24 us  [lap_periodic(): jnp.roll(grid_field, -1, which_axis)]
    all_to_all x1, waiting for transfers between devices: 0.01 us -> 11.1 us  [broadcast(): spread = lax.all_to_all(array, axis, 0, 0, tiled=True)]
    div x1, other arithmetic: 4.44 us -> 13.6 us  [shifted(): (hamiltonian_apply(extended, local_potential) - center * extended[:, 2:-2...]
    slice x8 -> x12, local copies, waits for them, and re-layouts: 13.6 us -> 21.6 us  [lap_periodic(): jnp.roll(grid_field, -2, which_axis)]
    unnamed x44 -> x24, local copies, waits for them, and re-layouts: 11.5 us -> 17.3 us
    add x1 -> x0, other arithmetic: 5.63 us -> none  [hamiltonian_apply(): return -0.5 * laplace + local_potential * interior]
    sub x1, other arithmetic: 3.42 us -> 8.8 us  [body(): filtered_wide = 2.0 * shifted(first_term, pot_wide[2:-2]) - wide[:, 4:-4]]
  transfers between devices with their start and end apart: 12 -> 12, of which waited for: 9 -> 8; matrix products, arithmetic and copies ran while one was open for 32% -> 19% of each run, Pallas kernels for 0% -> 0%
where the time goes in v3:
time: 207 us; the launch traced here: 205 us
  waiting for transfers between devices  69 us (33%)
  local copies, waits for them, and re-layouts  68 us (33%)
  starting transfers between devices  36.2 us (17%)
  other arithmetic  22.5 us (11%)
  matrix products  7.66 us (4%)
    ppermute x6, waiting for transfers between devices, shifted_to(): lax.ppermute(block, axis, [(i, (i + shift) % count) for i in range(count)])  32.3 us
    slice x12, local copies, waits for them, and re-layouts, lap_periodic(): jnp.roll(grid_field, -1, which_axis)  24 us
    slice x12, local copies, waits for them, and re-layouts, lap_periodic(): jnp.roll(grid_field, -2, which_axis)  21.6 us
    ppermute x6, starting transfers between devices, shifted_to(): lax.ppermute(block, axis, [(i, (i + shift) % count) for i in range(count)])  18.3 us
    unnamed x24, local copies, waits for them, and re-layouts  17.3 us
    ppermute x4, waiting for transfers between devices, doubling_sum(): lax.ppermute(array, axis, [(i, i ^ step) for i in range(count)])  15.2 us
    div x1, other arithmetic, shifted(): (hamiltonian_apply(extended, local_potential) - center * extended[:, 2:-2...  13.6 us
    all_to_all x1, waiting for transfers between devices, broadcast(): spread = lax.all_to_all(array, axis, 0, 0, tiled=True)  11.1 us
  transfers between devices with their start and end apart: 12, of which 8 were waited for; matrix products, arithmetic and copies ran while one was open for 19% of the time, Pallas kernels for 0%

profile of v3, /device:TPU:0, one launch (start us, length us, event | category | flops | bytes accessed | tf_op | source)
XLA Modules:
  0.0 204.9 jit_solution(5577192557345359909)
XLA Ops:
  0.6 2.8 %copy.14 = f32[64,4,8,128]{3,0,2,1:T(8,128)} copy(f32[64,4,8,128]{3,2,1,0:T(8,128)} %param.3) | data formatting | bytes 2097152 | tf_op args[0]
  3.5 1.5 collective-permute-start.1
  4.9 2.1 %fusion.125 = (f32[64,2,8,128]{3,0,2,1:T(8,128)S(1)}, f32[64,2,8,128]{3,0,2,1:T(8,128)}) fusion(f32[64,4,8,128]{3,0,2,1:T(8,128)} %copy.14), kind=kLoop, calls=%fused_computation.173 | loop fusion | bytes 2097152 | tf_op jit(solution)/shard_map/slice | solution.py:58
  7.0 1.9 collective-permute-start
  9.0 3.4 %collective-permute-start.2 = (f32[64,4,8,128]{3,0,2,1:T(8,128)}, f32[64,4,8,128]{3,0,2,1:T(8,128)}, u32[]{:S(2)}, u32[]{:S(2)}) collective-permute-start(f32[64,4,8,128]{3,0,2,1:T(8,128)} %copy.14), channel_id=1, source_target_pairs={{0,15},{1,0},{2,1},{3,2},{4,3},{5,4},{6,5},{7,6},{8,7},{9,8},{10,9... | collective-permute-start | bytes 3145736 | tf_op jit(solution)/shard_map/ppermute | solution.py:50
  12.5 5.5 %collective-permute-start.5 = (f32[4,8,128]{2,1,0:T(8,128)S(1)}, f32[4,8,128]{2,1,0:T(8,128)S(1)}, u32[]{:S(2)}, u32[]{:S(2)}) collective-permute-start(f32[4,8,128]{2,1,0:T(8,128)S(1)} %copy-done), channel_id=1, source_target_pairs={{0,15},{1,0},{2,1},{3,2},{4,3},{5,4},{6,5},{7,6},{8,7},{9,8},{10,9... | collective-permute-start | bytes 49160 | tf_op jit(solution)/shard_map/ppermute | solution.py:50
  18.6 32.1 %collective-permute-done.4 = f32[4,8,128]{2,1,0:T(8,128)S(1)} collective-permute-done((f32[4,8,128]{2,1,0:T(8,128)S(1)}, f32[4,8,128]{2,1,0:T(8,128)S(1)}, u32[]{:S(2)}, u32[]{:S(2)}) %collective-permute-start.4) | collective-permute-done | bytes 16416 | tf_op jit(solution)/shard_map/ppermute | solution.py:50
  50.7 5.9 %collective-permute-start.3 = (f32[64,2,8,128]{3,0,2,1:T(8,128)}, f32[64,2,8,128]{3,0,2,1:T(8,128)S(1)}, u32[]{:S(2)}, u32[]{:S(2)}) collective-permute-start(f32[64,2,8,128]{3,0,2,1:T(8,128)} %get-tuple-element.67), channel_id=1, source_target_pairs={{0,14},{1,15},{2,0},{3,1},{4,2},{5,3},{6,4},{7,5},{8,6},{9,7},{10,... | collective-permute-start | bytes 1572872 | tf_op jit(solution)/shard_map/ppermute | solution.py:50
  56.8 1.6 constant_dynamic-update-slice_fusion.2
  58.5 1.9 constant_dynamic-update-slice_fusion.1
  60.4 1.6 constant_dynamic-update-slice_fusion
  62.0 2.7 %fusion.115 = (f32[64,12,6,128]{3,0,2,1:T(8,128)}, f32[64,12,6,128]{3,0,2,1:T(8,128)}) fusion(f32[64,12,8,128]{3,0,2,1:T(8,128)S(1)} %get-tuple-element.58), kind=kLoop, calls=%fused_computation.163 | loop fusion | bytes 9437184 | tf_op jit(solution)/shard_map/jit(_roll_static)/slice | solution.py:28
  64.8 3.0 %fusion.113 = (f32[64,12,7,128]{3,0,2,1:T(8,128)}, f32[64,12,7,128]{3,0,2,1:T(8,128)}) fusion(f32[64,12,8,128]{3,0,2,1:T(8,128)S(1)} %get-tuple-element.58), kind=kLoop, calls=%fused_computation.161 | loop fusion | bytes 11010048 | tf_op jit(solution)/shard_map/jit(_roll_static)/slice | solution.py:29
  67.9 3.8 %fusion.111 = (f32[64,12,8,126]{3,0,2,1:T(8,128)}, f32[64,12,8,126]{3,0,2,1:T(8,128)}) fusion(f32[64,12,8,128]{3,0,2,1:T(8,128)S(1)} %get-tuple-element.58), kind=kLoop, calls=%fused_computation.159 | loop fusion | bytes 12386304 | tf_op jit(solution)/shard_map/jit(_roll_static)/slice | solution.py:28
  71.6 3.7 %fusion.112 = (f32[64,12,8,2]{3,0,2,1:T(8,128)}, f32[64,12,8,2]{3,0,2,1:T(8,128)}) fusion(f32[64,12,8,128]{3,0,2,1:T(8,128)S(1)} %get-tuple-element.58), kind=kLoop, calls=%fused_computation.160 | loop fusion | bytes 196608 | tf_op jit(solution)/shard_map/jit(_roll_static)/slice | solution.py:28
  75.3 3.7 %fusion.109 = (f32[64,12,8,127]{3,0,2,1:T(8,128)}, f32[64,12,8,127]{3,0,2,1:T(8,128)}) fusion(f32[64,12,8,128]{3,0,2,1:T(8,128)S(1)} %get-tuple-element.58), kind=kLoop, calls=%fused_computation.157 | loop fusion | bytes 12484608 | tf_op jit(solution)/shard_map/jit(_roll_static)/slice | solution.py:29
  79.1 3.8 %fusion.110 = (f32[64,12,8,1]{3,0,2,1:T(8,128)}, f32[64,12,8,1]{3,0,2,1:T(8,128)}) fusion(f32[64,12,8,128]{3,0,2,1:T(8,128)S(1)} %get-tuple-element.58), kind=kLoop, calls=%fused_computation.158 | loop fusion | bytes 98304 | tf_op jit(solution)/shard_map/jit(_roll_static)/slice | solution.py:29
  83.0 13.6 %fusion.8 = f32[64,12,8,128]{3,0,2,1:T(8,128)S(1)} fusion(f32[64,14,8,128]{3,0,2,1:T(8,128)S(1)} %constant_dynamic-update-slice_fusion.4, f32[64,14,8,128]{3,0,2,1:T(8,128)S(1)} %get-tuple-element.57, f32[64,12,6,128]{3,0,2,1:T(8,128)} %get-tuple-element.38, f32[64,12,2,128]{3,0,2,1:T(8,128)S(1)} %get-tuple-element.40, ...), kind=kLoop, calls=%fused_computation.9 | loop fusion | flops 27525120 | bytes 44089344 | tf_op jit(solution)/shard_map/div | solution.py:45
  96.6 2.0 fusion.107
  98.7 2.2 %fusion.105 = (f32[64,8,7,128]{3,0,2,1:T(8,128)}, f32[64,8,7,128]{3,0,2,1:T(8,128)}) fusion(f32[64,12,8,128]{3,0,2,1:T(8,128)S(1)} %fusion.8), kind=kLoop, calls=%fused_computation.153 | loop fusion | bytes 7340032 | tf_op jit(solution)/shard_map/jit(_roll_static)/slice | solution.py:29
  101.0 0.8 fusion.103
  101.8 2.8 %fusion.104 = (f32[64,8,8,2]{3,0,2,1:T(8,128)}, f32[64,8,8,2]{3,0,2,1:T(8,128)}) fusion(f32[64,12,8,128]{3,0,2,1:T(8,128)S(1)} %fusion.8), kind=kLoop, calls=%fused_computation.152 | loop fusion | bytes 131072 | tf_op jit(solution)/shard_map/jit(_roll_static)/slice | solution.py:28
  104.7 2.8 %fusion.101 = (f32[64,8,8,127]{3,0,2,1:T(8,128)}, f32[64,8,8,127]{3,0,2,1:T(8,128)}) fusion(f32[64,12,8,128]{3,0,2,1:T(8,128)S(1)} %fusion.8), kind=kLoop, calls=%fused_computation.149 | loop fusion | bytes 8323072 | tf_op jit(solution)/shard_map/jit(_roll_static)/slice | solution.py:29
  107.5 2.8 %fusion.102 = (f32[64,8,8,1]{3,0,2,1:T(8,128)}, f32[64,8,8,1]{3,0,2,1:T(8,128)}) fusion(f32[64,12,8,128]{3,0,2,1:T(8,128)S(1)} %fusion.8), kind=kLoop, calls=%fused_computation.150 | loop fusion | bytes 65536 | tf_op jit(solution)/shard_map/jit(_roll_static)/slice | solution.py:29
  110.2 8.8 %slice_subtract_fusion = f32[64,8,8,128]{3,0,2,1:T(8,128)S(1)} fusion(f32[64,12,8,128]{3,0,2,1:T(8,128)S(1)} %get-tuple-element.58, f32[64,12,8,128]{3,0,2,1:T(8,128)S(1)} %fusion.8, f32[64,8,6,128]{3,0,2,1:T(8,128)} %get-tuple-element.22, f32[64,8,2,128]{3,0,2,1:T(8,128)S(1)} %get-tuple-element.24, f32[64,8,2,128]{3,0,2,1:T(8,128)S(1)} %get-tuple-element.23, ...), kind=kLoop, calls=%fused_computation.24 | loop fusion | flops 18874368 | bytes 31490048 | tf_op jit(solution)/shard_map/sub | solution.py:67
  119.1 1.6 copy.24
  120.7 4.5 %all-to-all-start = ((f32[64,4,8,128]{3,2,1,0:T(8,128)}), f32[64,4,8,128]{3,2,1,0:T(8,128)S(1)}, u32[]{:S(2)}, u32[]{:S(2)}) async-start(f32[64,4,8,128]{3,2,1,0:T(8,128)} %copy.24), calls=%async_computation | async-start | bytes 2097152 | tf_op jit(solution)/shard_map/all_to_all | solution.py:13
  125.2 0.7 fusion.124
  126.0 1.4 fusion.123
  127.4 1.4 fusion.121
  128.8 1.7 fusion.119
  130.5 11.1 %all-to-all-done = f32[64,4,8,128]{3,2,1,0:T(8,128)S(1)} async-done(((f32[64,4,8,128]{3,2,1,0:T(8,128)}), f32[64,4,8,128]{3,2,1,0:T(8,128)S(1)}, u32[]{:S(2)}, u32[]{:S(2)}) %all-to-all-start) | async-done | bytes 1048608 | tf_op jit(solution)/shard_map/all_to_all | solution.py:13
  147.3 0.6 constant_dynamic-update-slice_fusion.20
  151.6 3.9 %all-to-all-start.1 = ((f32[64,4,8,128]{3,2,1,0:T(8,128)}), f32[64,4,8,128]{3,2,1,0:T(8,128)S(1)}, u32[]{:S(2)}, u32[]{:S(2)}) async-start(f32[64,4,8,128]{3,2,1,0:T(8,128)} %constant_dynamic-update-slice_fusion.14), calls=%async_computation.1 | async-start | bytes 2097152 | tf_op jit(solution)/shard_map/all_to_all | solution.py:15
  155.5 0.7 fusion.122
  156.2 1.7 fusion.120
  157.8 1.7 fusion.117
  159.6 1.8 fusion.118
  161.3 10.4 %all-to-all-done.1 = f32[64,4,8,128]{3,2,1,0:T(8,128)S(1)} async-done(((f32[64,4,8,128]{3,2,1,0:T(8,128)}), f32[64,4,8,128]{3,2,1,0:T(8,128)S(1)}, u32[]{:S(2)}, u32[]{:S(2)}) %all-to-all-start.1) | async-done | bytes 1048608 | tf_op jit(solution)/shard_map/all_to_all | solution.py:15
  171.7 1.5 fusion.39
  173.2 6.1 %fusion.37 = f32[1,64,64]{2,1,0:T(8,128)S(1)} fusion(f32[64,8,8,128]{3,0,2,1:T(8,128)S(1)} %slice_subtract_fusion, f32[64,4,6,128]{3,0,2,1:T(8,128)} %get-tuple-element.54, f32[64,4,2,128]{3,0,2,1:T(8,128)} %get-tuple-element.56, f32[64,4,2,128]{3,0,2,1:T(8,128)S(1)} %get-tuple-element.55, f32[64,4,6,128]{3,0,2,1:T(8,128)} %get-tuple-element.53, ...), kind=kOutput, calls=%fused_computation.51 | convolution fusion | flops 209719296 | bytes 14712832 | tf_op jit(solution)/shard_map/pc,bc->pb/dot_general | solution.py:77
  179.4 4.5 %collective-permute-start.6 = (f32[2,64,64]{2,1,0:T(8,128)S(1)}, f32[2,64,64]{2,1,0:T(8,128)S(1)}, u32[]{:S(2)}, u32[]{:S(2)}) collective-permute-start(f32[2,64,64]{2,1,0:T(8,128)S(1)} %pad_maximum_fusion), channel_id=1, source_target_pairs={{0,1},{1,0},{2,3},{3,2},{4,5},{5,4},{6,7},{7,6},{8,9},{9,8},{10,11... | collective-permute-start | bytes 98312 | tf_op jit(solution)/shard_map/ppermute | solution.py:22
  183.9 2.2 %collective-permute-done.6 = f32[2,64,64]{2,1,0:T(8,128)S(1)} collective-permute-done((f32[2,64,64]{2,1,0:T(8,128)S(1)}, f32[2,64,64]{2,1,0:T(8,128)S(1)}, u32[]{:S(2)}, u32[]{:S(2)}) %collective-permute-start.6) | collective-permute-done | bytes 32800 | tf_op jit(solution)/shard_map/ppermute | solution.py:22
  186.3 4.3 %collective-permute-done.7 = f32[2,64,64]{2,1,0:T(8,128)S(1)} collective-permute-done((f32[2,64,64]{2,1,0:T(8,128)S(1)}, f32[2,64,64]{2,1,0:T(8,128)S(1)}, u32[]{:S(2)}, u32[]{:S(2)}) %collective-permute-start.7) | collective-permute-done | bytes 32800 | tf_op jit(solution)/shard_map/ppermute | solution.py:22
  190.7 5.3 %collective-permute-done.8 = f32[2,64,64]{2,1,0:T(8,128)S(1)} collective-permute-done((f32[2,64,64]{2,1,0:T(8,128)S(1)}, f32[2,64,64]{2,1,0:T(8,128)S(1)}, u32[]{:S(2)}, u32[]{:S(2)}) %collective-permute-start.8) | collective-permute-done | bytes 32800 | tf_op jit(solution)/shard_map/ppermute | solution.py:22
  196.0 4.8 %collective-permute-start.9 = (f32[2,64,64]{2,1,0:T(8,128)S(1)}, f32[2,64,64]{2,1,0:T(8,128)S(1)}, u32[]{:S(2)}, u32[]{:S(2)}) collective-permute-start(f32[2,64,64]{2,1,0:T(8,128)S(1)} %add.162), channel_id=1, source_target_pairs={{0,8},{1,9},{2,10},{3,11},{4,12},{5,13},{6,14},{7,15},{8,0},{9,1},... | collective-permute-start | bytes 98312 | tf_op jit(solution)/shard_map/ppermute | solution.py:22
  200.8 3.4 %collective-permute-done.9 = f32[2,64,64]{2,1,0:T(8,128)S(1)} collective-permute-done((f32[2,64,64]{2,1,0:T(8,128)S(1)}, f32[2,64,64]{2,1,0:T(8,128)S(1)}, u32[]{:S(2)}, u32[]{:S(2)}) %collective-permute-start.9) | collective-permute-done | bytes 32800 | tf_op jit(solution)/shard_map/ppermute | solution.py:22
  204.2 0.6 slice_bitcast_fusion
  (41 shorter events, 10.3 us)
Async XLA Ops:
  0.6 11.7 %copy-start = (f32[4,8,128]{2,1,0:T(8,128)S(1)}, f32[4,8,128]{2,1,0:T(8,128)}, u32[]{:S(2)}) copy-start(f32[4,8,128]{2,1,0:T(8,128)} %param.4) | copy-start | bytes 49156
  3.5 53.4 %collective-permute-start.1 = (f32[64,4,8,128]{3,0,2,1:T(8,128)}, f32[64,4,8,128]{3,0,2,1:T(8,128)}, u32[]{:S(2)}, u32[]{:S(2)}) collective-permute-start(f32[64,4,8,128]{3,0,2,1:T(8,128)} %copy.14), channel_id=1, source_target_pairs={{0,1},{1,2},{2,3},{3,4},{4,5},{5,6},{6,7},{7,8},{8,9},{9,10},{10,1... | collective-permute-start | bytes 3145736 | tf_op jit(solution)/shard_map/ppermute | solution.py:50
  7.0 49.7 %collective-permute-start = (f32[64,2,8,128]{3,0,2,1:T(8,128)S(1)}, f32[64,2,8,128]{3,0,2,1:T(8,128)S(1)}, u32[]{:S(2)}, u32[]{:S(2)}) collective-permute-start(f32[64,2,8,128]{3,0,2,1:T(8,128)S(1)} %get-tuple-element.66), channel_id=1, source_target_pairs={{0,2},{1,3},{2,4},{3,5},{4,6},{5,7},{6,8},{7,9},{8,10},{9,11},{10,... | collective-permute-start | bytes 1572872 | tf_op jit(solution)/shard_map/ppermute | solution.py:50
  9.0 51.4 %collective-permute-start.2 = (f32[64,4,8,128]{3,0,2,1:T(8,128)}, f32[64,4,8,128]{3,0,2,1:T(8,128)}, u32[]{:S(2)}, u32[]{:S(2)}) collective-permute-start(f32[64,4,8,128]{3,0,2,1:T(8,128)} %copy.14), channel_id=1, source_target_pairs={{0,15},{1,0},{2,1},{3,2},{4,3},{5,4},{6,5},{7,6},{8,7},{9,8},{10,9... | collective-permute-start | bytes 3145736 | tf_op jit(solution)/shard_map/ppermute | solution.py:50
  12.3 38.4 %collective-permute-start.4 = (f32[4,8,128]{2,1,0:T(8,128)S(1)}, f32[4,8,128]{2,1,0:T(8,128)S(1)}, u32[]{:S(2)}, u32[]{:S(2)}) collective-permute-start(f32[4,8,128]{2,1,0:T(8,128)S(1)} %copy-done), channel_id=1, source_target_pairs={{0,1},{1,2},{2,3},{3,4},{4,5},{5,6},{6,7},{7,8},{8,9},{9,10},{10,1... | collective-permute-start | bytes 49160 | tf_op jit(solution)/shard_map/ppermute | solution.py:50
  12.5 44.3 %collective-permute-start.5 = (f32[4,8,128]{2,1,0:T(8,128)S(1)}, f32[4,8,128]{2,1,0:T(8,128)S(1)}, u32[]{:S(2)}, u32[]{:S(2)}) collective-permute-start(f32[4,8,128]{2,1,0:T(8,128)S(1)} %copy-done), channel_id=1, source_target_pairs={{0,15},{1,0},{2,1},{3,2},{4,3},{5,4},{6,5},{7,6},{8,7},{9,8},{10,9... | collective-permute-start | bytes 49160 | tf_op jit(solution)/shard_map/ppermute | solution.py:50
  50.7 32.2 %collective-permute-start.3 = (f32[64,2,8,128]{3,0,2,1:T(8,128)}, f32[64,2,8,128]{3,0,2,1:T(8,128)S(1)}, u32[]{:S(2)}, u32[]{:S(2)}) collective-permute-start(f32[64,2,8,128]{3,0,2,1:T(8,128)} %get-tuple-element.67), channel_id=1, source_target_pairs={{0,14},{1,15},{2,0},{3,1},{4,2},{5,3},{6,4},{7,5},{8,6},{9,7},{10,... | collective-permute-start | bytes 1572872 | tf_op jit(solution)/shard_map/ppermute | solution.py:50
  120.7 21.0 %all-to-all-start = ((f32[64,4,8,128]{3,2,1,0:T(8,128)}), f32[64,4,8,128]{3,2,1,0:T(8,128)S(1)}, u32[]{:S(2)}, u32[]{:S(2)}) async-start(f32[64,4,8,128]{3,2,1,0:T(8,128)} %copy.24), calls=%async_computation | async-start | bytes 2097152 | tf_op jit(solution)/shard_map/all_to_all | solution.py:13
  151.6 20.1 %all-to-all-start.1 = ((f32[64,4,8,128]{3,2,1,0:T(8,128)}), f32[64,4,8,128]{3,2,1,0:T(8,128)S(1)}, u32[]{:S(2)}, u32[]{:S(2)}) async-start(f32[64,4,8,128]{3,2,1,0:T(8,128)} %constant_dynamic-update-slice_fusion.14), calls=%async_computation.1 | async-start | bytes 2097152 | tf_op jit(solution)/shard_map/all_to_all | solution.py:15
  179.4 6.8 %collective-permute-start.6 = (f32[2,64,64]{2,1,0:T(8,128)S(1)}, f32[2,64,64]{2,1,0:T(8,128)S(1)}, u32[]{:S(2)}, u32[]{:S(2)}) collective-permute-start(f32[2,64,64]{2,1,0:T(8,128)S(1)} %pad_maximum_fusion), channel_id=1, source_target_pairs={{0,1},{1,0},{2,3},{3,2},{4,5},{5,4},{6,7},{7,6},{8,9},{9,8},{10,11... | collective-permute-start | bytes 98312 | tf_op jit(solution)/shard_map/ppermute | solution.py:22
  186.2 4.4 %collective-permute-start.7 = (f32[2,64,64]{2,1,0:T(8,128)S(1)}, f32[2,64,64]{2,1,0:T(8,128)S(1)}, u32[]{:S(2)}, u32[]{:S(2)}) collective-permute-start(f32[2,64,64]{2,1,0:T(8,128)S(1)} %fusion.98), channel_id=1, source_target_pairs={{0,2},{1,3},{2,0},{3,1},{4,6},{5,7},{6,4},{7,5},{8,10},{9,11},{10,... | collective-permute-start | bytes 98312 | tf_op jit(solution)/shard_map/ppermute | solution.py:22
  190.6 5.4 %collective-permute-start.8 = (f32[2,64,64]{2,1,0:T(8,128)S(1)}, f32[2,64,64]{2,1,0:T(8,128)S(1)}, u32[]{:S(2)}, u32[]{:S(2)}) collective-permute-start(f32[2,64,64]{2,1,0:T(8,128)S(1)} %fusion.126), channel_id=1, source_target_pairs={{0,4},{1,5},{2,6},{3,7},{4,0},{5,1},{6,2},{7,3},{8,12},{9,13},{10,... | collective-permute-start | bytes 98312 | tf_op jit(solution)/shard_map/ppermute | solution.py:22
  196.0 8.3 %collective-permute-start.9 = (f32[2,64,64]{2,1,0:T(8,128)S(1)}, f32[2,64,64]{2,1,0:T(8,128)S(1)}, u32[]{:S(2)}, u32[]{:S(2)}) collective-permute-start(f32[2,64,64]{2,1,0:T(8,128)S(1)} %add.162), channel_id=1, source_target_pairs={{0,8},{1,9},{2,10},{3,11},{4,12},{5,13},{6,14},{7,15},{8,0},{9,1},... | collective-permute-start | bytes 98312 | tf_op jit(solution)/shard_map/ppermute | solution.py:22
